TPU v7x, 128 devices: a whole 4x4x4 slice. The times are simulated.
128 devices in a mesh: sample: 8 (over x, y_hi), landmark: 16 (over z, y_lo, core).
Axes of the slice: x: 4, y: 4 (y_hi: 2, y_lo: 2; y = y_hi * 2 + y_lo), z: 4, core: 2. Of those that a mesh axis runs over, the one named last changes fastest.
Arguments:
- summaries: bfloat16 [16384, 1024], P('sample', 'landmark'), may hold values from -12 to 12
- row_level: int32 [16384], P('sample'), may hold values from 0 to 3
- pool: bfloat16 [32768, 1024], P('landmark'), may hold values from -6 to 6
- pool_level: int32 [32768], P('landmark'), may hold values from 0 to 3
- landmark_index: int32 [16384], P('landmark'), may hold values from 0 to 2047, as said below
- level_scale: float32 [4], replicated, may hold values from 1.2 to 2.4
- targets: bfloat16 [16384, 256], P('sample'), may hold values from -6 to 6
Outputs:
- weights: float32 [16384, 256], P('landmark')
- residual: float32 [16384, 256], P('landmark')
Inputs may be any that keep to these rules, and one draw needn't show every extreme that they name: Landmark j is pool row (j // 1024) * 2048 + landmark_index[j], a row of the pool block of its own landmark group; indices may repeat.
All inputs are finite; a program needn't handle non-finite values.
Results may differ from a plain program's by a relative error of at most 0.012.
Values may be sent and summed in bfloat16 or wider, within the bound.
No kernel may reach another device: no remote copies, remote signals or barrier semaphores. Data moves between devices by JAX's collectives and lax.ppermute only.
A program may use at most 64 MiB of HBM per device.

v0:
```python
import math

import jax
import jax.numpy as jnp
from jax import lax
from jax.sharding import PartitionSpec as P

ITERS = 2


ridge = 0.5


def level_values(level_ids, level_table):
    onehot = level_ids[:, None] == jnp.arange(level_table.shape[0], dtype=jnp.int32)[None, :]
    return jnp.sum(
        jnp.where(onehot, level_table[None, :], jnp.zeros_like(level_table)[None, :]), axis=1
    )


def raw_block(summary_rows, row_factor, anchors, anchor_factor):
    scores = jnp.dot(summary_rows, anchors.T, preferred_element_type=jnp.float32)
    return jnp.exp(scores * row_factor[:, None] * anchor_factor[None, :])


def kernel_block(summary_rows, row_factor, anchors, anchor_factor, column_mean):
    raw = raw_block(summary_rows, row_factor, anchors, anchor_factor)
    return (raw - column_mean[None, :]).astype(jnp.bfloat16)


def column_norm(residual):
    return lax.psum(jnp.sum(residual * residual, axis=0), "landmark")


def on_device(summaries, row_level, pool, pool_level, landmark_index, level_scale, targets):
    row_count = summaries.shape[0]
    n_rows = row_count * lax.axis_size("sample")
    gathered = lax.all_gather(summaries, "landmark", axis=1, tiled=True)
    feature_count = gathered.shape[1]
    anchors = jnp.take(pool, landmark_index, axis=0)
    anchor_level = jnp.take(pool_level, landmark_index, axis=0)
    row_factor = 1.0 / math.sqrt(feature_count) / level_values(row_level, level_scale)
    anchor_factor = 1.0 / level_values(anchor_level, level_scale)
    raw_first = raw_block(gathered, row_factor, anchors, anchor_factor)
    column_mean = lax.psum(jnp.sum(raw_first, axis=0), "sample") / n_rows
    kernel_first = (raw_first - column_mean[None, :]).astype(jnp.bfloat16)
    rhs_part = jnp.dot(kernel_first.T, targets, preferred_element_type=jnp.float32)
    rhs = lax.psum(rhs_part, "sample") / math.sqrt(n_rows)
    weights = jnp.zeros_like(rhs)
    residual = rhs
    direction = rhs
    norm_now = column_norm(residual)
    for iteration in range(ITERS):
        kernel = kernel_block(gathered, row_factor, anchors, anchor_factor, column_mean)
        direction_half = direction.astype(jnp.bfloat16)
        row_total = lax.psum(
            jnp.dot(kernel, direction_half, preferred_element_type=jnp.float32), "landmark"
        )
        row_half = row_total.astype(jnp.bfloat16)
        column_part = jnp.dot(kernel.T, row_half, preferred_element_type=jnp.float32)
        image = lax.psum(column_part, "sample") / n_rows + ridge * direction
        curvature = lax.psum(jnp.sum(direction * image, axis=0), "landmark")
        step_size = norm_now / curvature
        weights = weights + step_size * direction
        residual = residual - step_size * image
        norm_next = column_norm(residual)
        direction = residual + norm_next / norm_now * direction
        norm_now = norm_next
    return (weights, residual)


def solution(mesh):
    return jax.shard_map(
        on_device,
        mesh=mesh,
        in_specs=(
            P("sample", "landmark"),
            P("sample"),
            P("landmark", None),
            P("landmark"),
            P("landmark"),
            P(),
            P("sample", None),
        ),
        out_specs=(P("landmark", None), P("landmark", None)),
        check_vma=False,
    )
```

profile of v0, /device:TPU:0, one launch (start us, length us, event | category | flops | bytes accessed | tf_op | source)
XLA Modules:
  0.0 605.8 jit_solution(15013070073280404615)
XLA Ops:
  7.2 0.0 copy-start
  7.2 0.0 all-gather.2.cloned.1.call-start
  7.2 0.7 all-gather.2.cloned.1.call-update
  7.9 0.0 all-reduce.7.cloned.1.call-start
  8.0 0.7 fusion.13
  8.7 5.7 gather_fusion.1
  14.4 0.0 copy-start.4
  14.4 0.0 copy-start.6
  14.4 0.0 copy-start.5
  14.4 7.7 %gather_fusion = bf16[1024,1024]{1,0:T(8,128)(2,1)S(1)} fusion(bf16[2048,1024]{1,0:T(8,128)(2,1)} %param.9, s32[1024]{0:T(1024)S(1)} %fusion.13), kind=kCustom, calls=%fused_computation | custom fusion | bytes 4198400 | tf_op jit(solution)/shard_map/jit(_take)/gather | solution.py:40
  22.2 0.0 copy-done.4
  22.2 0.0 copy-done.6
  22.2 0.1 select_reduce_fusion.1
  22.3 0.0 copy-done.5
  22.3 0.1 select_reduce_fusion
  22.4 27.2 %all-gather.2.cloned.1.call-done = bf16[2048,1024]{0,1:T(8,128)(2,1)} async-done(((bf16[2048,64]{0,1:T(8,128)(2,1)}), bf16[2048,1024]{0,1:T(8,128)(2,1)}) %all-gather.2.cloned.1.call-update) | async-done | bytes 4194320 | tf_op jit(solution)/shard_map/all_gather | solution.py:38
  49.6 9.6 %fusion = (f32[1024]{0:T(1024)S(1)}, f32[1024,2048]{1,0:T(8,128)}) fusion(f32[1024]{0:T(1024)S(1)} %broadcast_divide_fusion.1, f32[2048]{0:T(1024)S(1)} %broadcast_divide_fusion, bf16[2048,1024]{0,1:T(8,128)(2,1)} %all-gather.2.cloned.1.call-done, bf16[1024,1024]{1,0:T(8,128)(2,1)S(1)} %gather_fusion, pred[1024]{0:T(1024)(128)(4,1)S(1)} %get-tuple-element.9), kind=kOutput, calls=%fused_computation.4 | convolution fusion | flops 4302306304 | bytes 14697472 | tf_op jit(solution)/shard_map/dot_general | solution.py:22
  59.2 23.8 %psum.70 = f32[1024]{0:T(1024)S(1)} all-reduce(f32[1024]{0:T(1024)S(1)} %get-tuple-element.12), channel_id=1, replica_groups=mesh['sample'=8,'landmark'=16] {'sample'}, use_global_device_ids=true, to_apply=%region_3.4 | all-reduce | flops 1024 | bytes 8192 | tf_op jit(solution)/shard_map/psum | solution.py:45
  83.1 4.3 subtract_convert_fusion
  87.4 0.0 copy-start.3
  87.4 1.9 copy-done.3
  89.3 0.0 copy-done
  89.3 2.2 fusion.16
  91.5 0.0 all-reduce.7.cloned.1.call-update
  91.6 0.0 all-reduce.9.cloned.1.call-start
  91.6 84.3 %all-reduce.7.cloned.1.call-done = f32[1024,256]{1,0:T(8,128)} async-done(((f32[1024,256]{1,0:T(8,128)}), f32[1024,256]{1,0:T(8,128)}) %all-reduce.7.cloned.1.call-update) | async-done | bytes 1048592 | tf_op jit(solution)/shard_map/psum | solution.py:48
  176.0 3.8 fusion.9
  179.8 72.8 %all-reduce.12 = bf16[2048,256]{1,0:T(8,128)(2,1)} all-reduce(f32[2048,256]{1,0:T(8,128)S(1)} %fusion.9), channel_id=1, replica_groups=mesh['sample'=8,'landmark'=16] {'landmark'}, use_global_device_ids=true, to_apply=%region_7.8 | all-reduce | flops 524288 | bytes 3145728 | tf_op jit(solution)/shard_map/psum | solution.py:56
  252.6 0.0 copy-start.1
  252.6 4.8 fusion.18
  257.4 0.0 all-reduce.9.cloned.1.call-update
  257.4 0.0 all-reduce.11.cloned.1.call-start
  257.5 84.7 %all-reduce.9.cloned.1.call-done = f32[1024,256]{1,0:T(8,128)} async-done(((f32[1024,256]{1,0:T(8,128)}), f32[1024,256]{1,0:T(8,128)}) %all-reduce.9.cloned.1.call-update) | async-done | bytes 1048592 | tf_op jit(solution)/shard_map/psum | solution.py:61
  342.1 0.0 copy-done.1
  342.1 0.0 copy-start.2
  342.1 1.6 multiply_reduce_fusion.2
  343.7 27.1 %all-reduce = (f32[256]{0:T(256)S(1)}, f32[256]{0:T(256)S(1)}) all-reduce(f32[256]{0:T(256)S(1)} %get-tuple-element.3, f32[256]{0:T(256)S(1)} %get-tuple-element.2), channel_id=1, replica_groups=mesh['sample'=8,'landmark'=16] {'landmark'}, use_global_device_ids=true, to_apply=%region_6.7 | all-reduce | flops 512 | bytes 4096 | tf_op jit(solution)/shard_map/psum | solution.py:32
  370.9 1.5 multiply_reduce_fusion.1
  372.4 27.1 %psum.76 = f32[256]{0:T(256)S(1)} all-reduce(f32[256]{0:T(256)S(1)} %multiply_reduce_fusion.1), channel_id=1, replica_groups=mesh['sample'=8,'landmark'=16] {'landmark'}, use_global_device_ids=true, to_apply=%region_12.13 | all-reduce | flops 256 | bytes 2048 | tf_op jit(solution)/shard_map/psum | solution.py:32
  399.6 0.0 copy-done.2
  399.6 4.9 fusion.10
  404.5 72.9 %all-reduce.13 = bf16[2048,256]{1,0:T(8,128)(2,1)} all-reduce(f32[2048,256]{1,0:T(8,128)} %fusion.10), channel_id=1, replica_groups=mesh['sample'=8,'landmark'=16] {'landmark'}, use_global_device_ids=true, to_apply=%region_13.14 | all-reduce | flops 524288 | bytes 3145728 | tf_op jit(solution)/shard_map/psum | solution.py:56
  477.4 4.7 fusion.17
  482.1 0.0 all-reduce.11.cloned.1.call-update
  482.2 85.2 %all-reduce.11.cloned.1.call-done = f32[1024,256]{1,0:T(8,128)} async-done(((f32[1024,256]{1,0:T(8,128)}), f32[1024,256]{1,0:T(8,128)}) %all-reduce.11.cloned.1.call-update) | async-done | bytes 1048592 | tf_op jit(solution)/shard_map/psum | solution.py:61
  567.3 1.7 multiply_reduce_fusion
  569.0 27.1 %psum.79 = f32[256]{0:T(256)S(1)} all-reduce(f32[256]{0:T(256)S(1)} %multiply_reduce_fusion), channel_id=1, replica_groups=mesh['sample'=8,'landmark'=16] {'landmark'}, use_global_device_ids=true, to_apply=%region_16.17 | all-reduce | flops 256 | bytes 2048 | tf_op jit(solution)/shard_map/psum | solution.py:62
  596.2 3.1 multiply_subtract_fusion
  (7 shorter events, 0.0 us)
Async XLA Ops:
  7.2 82.2 %copy-start = (bf16[2048,256]{1,0:T(8,128)(2,1)S(1)}, bf16[2048,256]{1,0:T(8,128)(2,1)}, u32[]{:S(2)}) copy-start(bf16[2048,256]{1,0:T(8,128)(2,1)} %param.13) | copy-start | bytes 3145732
  7.2 42.4 %all-gather.2.cloned.1.call-start = ((), (), s32[]{:S(2)}) async-start(), calls=%async_computation | async-start | bytes 4456448 | tf_op jit(solution)/shard_map/all_gather | solution.py:38
  7.9 168.0 %all-reduce.7.cloned.1.call-start = ((), (), s32[]{:S(2)}) async-start(), calls=%async_computation.1 | async-start | bytes 2097152 | tf_op jit(solution)/shard_map/psum | solution.py:48
  14.4 7.8 %copy-start.4 = (s32[1024]{0:T(1024)S(1)}, s32[1024]{0:T(1024)}, u32[]{:S(2)}) copy-start(s32[1024]{0:T(1024)} %param.11) | copy-start | bytes 12292
  14.4 7.8 %copy-start.6 = (f32[4]{0:T(128)S(1)}, f32[4]{0:T(128)}, u32[]{:S(2)}) copy-start(f32[4]{0:T(128)} %param.12) | copy-start | bytes 52
  14.4 7.9 %copy-start.5 = (s32[2048]{0:T(1024)S(1)}, s32[2048]{0:T(1024)}, u32[]{:S(2)}) copy-start(s32[2048]{0:T(1024)} %param.8) | copy-start | bytes 24580
  87.4 1.9 copy-start.3
  91.6 250.6 %all-reduce.9.cloned.1.call-start = ((), (), s32[]{:S(2)}) async-start(), calls=%async_computation.2 | async-start | bytes 2097152 | tf_op jit(solution)/shard_map/psum | solution.py:61
  252.6 89.6 %copy-start.1 = (f32[1024,256]{1,0:T(8,128)S(1)}, f32[1024,256]{1,0:T(8,128)}, u32[]{:S(2)}) copy-start(f32[1024,256]{1,0:T(8,128)} %all-reduce.7.cloned.1.call-done) | copy-start | bytes 3145732
  257.4 309.9 %all-reduce.11.cloned.1.call-start = ((), (), s32[]{:S(2)}) async-start(), calls=%async_computation.3 | async-start | bytes 2097152 | tf_op jit(solution)/shard_map/psum | solution.py:61
  342.1 57.4 %copy-start.2 = (f32[1024,256]{1,0:T(8,128)S(1)}, f32[1024,256]{1,0:T(8,128)}, u32[]{:S(2)}) copy-start(f32[1024,256]{1,0:T(8,128)} %all-reduce.9.cloned.1.call-done) | copy-start | bytes 3145732
Sparse Core Ops, SparseCore 0:
  9.7 39.8 all-gather.1
  91.7 84.2 all-reduce.6
  257.5 84.5 all-reduce.8
  482.3 85.0 all-reduce.10
where the time goes:
time: 607 us; the launch traced here: 606 us
  waiting for transfers between devices  282 us (46%)
  blocking collectives  251 us (41%)
  matrix products  30.1 us (5%)
  local copies, waits for them, and re-layouts  15.4 us (3%)
  between operations  13.9 us (2%)
  other arithmetic  13.1 us (2%)
    psum x2, waiting for transfers between devices, on_device(): image = lax.psum(column_part, 'sample') / n_rows + ridge * direction  170 us
    psum x2, blocking collectives, on_device(): lax.psum(jnp.dot(kernel, direction_half, preferred_element_type=jnp.float...  146 us
    psum x1, waiting for transfers between devices, on_device(): rhs = lax.psum(rhs_part, 'sample') / math.sqrt(n_rows)  84.3 us
    psum x2, blocking collectives, column_norm(): return lax.psum(jnp.sum(residual * residual, axis=0), 'landmark')  54.3 us
    all_gather x1, waiting for transfers between devices, on_device(): gathered = lax.all_gather(summaries, 'landmark', axis=1, tiled=True)  27.2 us
    psum x1, blocking collectives, on_device(): curvature = lax.psum(jnp.sum(direction * image, axis=0), 'landmark')  27.1 us
    psum x1, blocking collectives, on_device(): column_mean = lax.psum(jnp.sum(raw_first, axis=0), 'sample') / n_rows  23.8 us
  transfers between devices with their start and end apart: 4, of which 4 were waited for; matrix products, arithmetic and copies ran while one was open for 2% of the time, Pallas kernels for 0%

commit v1 on v0

v1 whole, which is shorter than its diff:
```python
import math

import jax
import jax.numpy as jnp
from jax import lax
from jax.sharding import PartitionSpec as P

ITERS = 2


ridge = 0.5


def level_values(level_ids, level_table):
    onehot = level_ids[:, None] == jnp.arange(level_table.shape[0], dtype=jnp.int32)[None, :]
    return jnp.sum(
        jnp.where(onehot, level_table[None, :], jnp.zeros_like(level_table)[None, :]), axis=1
    )


def raw_block(summary_rows, row_factor, anchors, anchor_factor):
    scores = jnp.dot(summary_rows, anchors.T, preferred_element_type=jnp.float32)
    return jnp.exp(scores * row_factor[:, None] * anchor_factor[None, :])


def partner_bits(size, order):
    bits = [b for b in order if b < size]
    assert sorted(bits) == [1 << i for i in range(size.bit_length() - 1)]
    return bits


def butterfly_sum(x, axis, bits):
    size = lax.axis_size(axis)
    for k in bits:
        perm = [(i, i ^ k) for i in range(size)]
        x = x + lax.ppermute(x, axis, perm)
    return x


def halving_sum(x, extra, axis, bits, gather_dtype):
    size = lax.axis_size(axis)
    index = lax.axis_index(axis)
    for k in bits:
        perm = [(i, i ^ k) for i in range(size)]
        half = x.shape[0] // 2
        mine = (index // k) % 2
        keep = lax.dynamic_slice_in_dim(x, mine * half, half, axis=0)
        send = lax.dynamic_slice_in_dim(x, (1 - mine) * half, half, axis=0)
        got, got_extra = lax.ppermute((send, extra), axis, perm)
        x = keep + got
        extra = extra + got_extra
    x = x.astype(gather_dtype)
    for k in reversed(bits):
        perm = [(i, i ^ k) for i in range(size)]
        part = x.shape[0]
        mine = (index // k) % 2
        got = lax.ppermute(x, axis, perm)
        whole = jnp.zeros((2 * part,) + x.shape[1:], x.dtype)
        whole = lax.dynamic_update_slice_in_dim(whole, x, mine * part, axis=0)
        x = lax.dynamic_update_slice_in_dim(whole, got, (1 - mine) * part, axis=0)
    return x, extra


def on_device(summaries, row_level, pool, pool_level, landmark_index, level_scale, targets):
    sample_bits = partner_bits(lax.axis_size("sample"), (2, 1, 4, 8, 16, 32, 64))
    landmark_bits = partner_bits(lax.axis_size("landmark"), (1, 2, 4, 8, 16, 32, 64))
    row_count = summaries.shape[0]
    n_rows = row_count * lax.axis_size("sample")
    gathered = lax.all_gather(summaries, "landmark", axis=1, tiled=True)
    feature_count = gathered.shape[1]
    anchors = jnp.take(pool, landmark_index, axis=0)
    anchor_level = jnp.take(pool_level, landmark_index, axis=0)
    row_factor = 1.0 / math.sqrt(feature_count) / level_values(row_level, level_scale)
    anchor_factor = 1.0 / level_values(anchor_level, level_scale)
    raw = raw_block(gathered, row_factor, anchors, anchor_factor)
    column_mean = butterfly_sum(jnp.sum(raw, axis=0), "sample", sample_bits) / n_rows
    kernel = (raw - column_mean[None, :]).astype(jnp.bfloat16)
    rhs_part = jnp.dot(kernel.T, targets, preferred_element_type=jnp.float32)
    rhs_total, _ = halving_sum(rhs_part, jnp.zeros((1,), jnp.float32), "sample", sample_bits, jnp.float32)
    rhs = rhs_total / math.sqrt(n_rows)
    weights = jnp.zeros_like(rhs)
    residual = rhs
    direction = rhs
    norm_now = None
    for iteration in range(ITERS):
        direction_half = direction.astype(jnp.bfloat16)
        row_part = jnp.dot(kernel, direction_half, preferred_element_type=jnp.float32)
        sums = [jnp.sum(direction * direction, axis=0)]
        if norm_now is None:
            sums.append(jnp.sum(residual * residual, axis=0))
        row_half, landmark_sums = halving_sum(
            row_part, jnp.concatenate(sums), "landmark", landmark_bits, jnp.bfloat16
        )
        column_count = direction.shape[1]
        direction_square = landmark_sums[:column_count]
        if norm_now is None:
            norm_now = landmark_sums[column_count:]
        row_square = jnp.sum(jnp.square(row_half.astype(jnp.float32)), axis=0)
        column_part = jnp.dot(kernel.T, row_half, preferred_element_type=jnp.float32)
        column_total, row_square_total = halving_sum(
            column_part, row_square, "sample", sample_bits, jnp.float32
        )
        image = column_total / n_rows + ridge * direction
        curvature = row_square_total / n_rows + ridge * direction_square
        step_size = norm_now / curvature
        weights = weights + step_size * direction
        residual = residual - step_size * image
        norm_next = butterfly_sum(jnp.sum(residual * residual, axis=0), "landmark", landmark_bits)
        direction = residual + norm_next / norm_now * direction
        norm_now = norm_next
    return (weights, residual)


def solution(mesh):
    return jax.shard_map(
        on_device,
        mesh=mesh,
        in_specs=(
            P("sample", "landmark"),
            P("sample"),
            P("landmark", None),
            P("landmark"),
            P("landmark"),
            P(),
            P("sample", None),
        ),
        out_specs=(P("landmark", None), P("landmark", None)),
        check_vma=False,
    )
```

time: 607 us -> 397 us (0.65)
  blocking collectives: 251 us -> 0 us
  starting transfers between devices: 0.16 us -> 93.8 us
  waiting for transfers between devices: 282 us -> 239 us
  matrix products: 30.1 us -> 19.7 us
    psum x3 -> x0, waiting for transfers between devices: 254 us -> none  [the longest x2 170 us: on_device(): image = lax.psum(column_part, 'sample') / n_rows + ridge * direction]
    psum x6 -> x0, blocking collectives: 251 us -> none  [the longest x2 146 us: on_device(): lax.psum(jnp.dot(kernel, direction_half, preferred_element_type=jnp.float...]
    ppermute x0 -> x55, waiting for transfers between devices: none -> 212 us  [the longest x31 143 us: halving_sum(): got, got_extra = lax.ppermute((send, extra), axis, perm)]
    ppermute x0 -> x55, starting transfers between devices: none -> 93.8 us  [the longest x31 50.1 us: halving_sum(): got, got_extra = lax.ppermute((send, extra), axis, perm)]
    dot_general x2, matrix products: 9.51 us -> 2.53 us  [on_device(): jnp.dot(kernel.T, row_half, preferred_element_type=jnp.float32)]
  transfers between devices with their start and end apart: 4 -> 56, of which waited for: 4 -> 49; matrix products, arithmetic and copies ran while one was open for 2% -> 4% of each run, Pallas kernels for 0% -> 0%
where the time goes in v1:
time: 397 us
  waiting for transfers between devices  239 us (60%)
  starting transfers between devices  93.8 us (24%)
  matrix products  19.7 us (5%)
  local copies, waits for them, and re-layouts  18.6 us (5%)
  between operations  14.8 us (4%)
  other arithmetic  10.8 us (3%)
    ppermute x31, waiting for transfers between devices, halving_sum(): got, got_extra = lax.ppermute((send, extra), axis, perm)  143 us
    ppermute x17, waiting for transfers between devices, halving_sum(): got = lax.ppermute(x, axis, perm)  54.5 us
    ppermute x31, starting transfers between devices, halving_sum(): got, got_extra = lax.ppermute((send, extra), axis, perm)  50.1 us
    ppermute x17, starting transfers between devices, halving_sum(): got = lax.ppermute(x, axis, perm)  31.4 us
    all_gather x1, waiting for transfers between devices, on_device(): gathered = lax.all_gather(summaries, 'landmark', axis=1, tiled=True)  26.2 us
    ppermute x7, waiting for transfers between devices, butterfly_sum(): x = x + lax.ppermute(x, axis, perm)  15 us
    ppermute x7, starting transfers between devices, butterfly_sum(): x = x + lax.ppermute(x, axis, perm)  12.3 us
    dot_general x1, matrix products, raw_block(): jnp.dot(summary_rows, anchors.T, preferred_element_type=jnp.float32)  10.9 us
  transfers between devices with their start and end apart: 56, of which 49 were waited for; matrix products, arithmetic and copies ran while one was open for 4% of the time, Pallas kernels for 0%

profile of v1, /device:TPU:0, one launch (start us, length us, event | category | flops | bytes accessed | tf_op | source)
XLA Modules:
  0.0 397.0 jit_solution(5923915539810918523)
XLA Ops:
  8.6 5.7 %gather_fusion.1 = s32[1024]{0:T(1024)S(1)} fusion(s32[2048]{0:T(1024)} %param.10, s32[1024]{0:T(1024)S(1)} %fusion.9), kind=kCustom, calls=%fused_computation.1 | custom fusion | bytes 12288 | tf_op jit(solution)/shard_map/jit(_take)/gather | solution.py:72
  14.4 8.8 %gather_fusion = bf16[1024,1024]{1,0:T(8,128)(2,1)} fusion(bf16[2048,1024]{1,0:T(8,128)(2,1)} %param.9, s32[1024]{0:T(1024)S(1)} %fusion.9), kind=kCustom, calls=%fused_computation | custom fusion | bytes 4198400 | tf_op jit(solution)/shard_map/jit(_take)/gather | solution.py:71
  23.4 26.2 %all-gather.2.cloned.1.call-done = bf16[2048,1024]{0,1:T(8,128)(2,1)} async-done(((bf16[2048,64]{0,1:T(8,128)(2,1)}), bf16[2048,1024]{0,1:T(8,128)(2,1)}) %all-gather.2.cloned.1.call-update) | async-done | bytes 4194320 | tf_op jit(solution)/shard_map/all_gather | solution.py:69
  49.6 10.9 %fusion = (f32[1024]{0:T(1024)S(1)}, f32[1024,2048]{1,0:T(8,128)}) fusion(f32[1024]{0:T(1024)S(1)} %broadcast_divide_fusion.1, f32[2048]{0:T(1024)S(1)} %broadcast_divide_fusion, bf16[2048,1024]{0,1:T(8,128)(2,1)} %all-gather.2.cloned.1.call-done, bf16[1024,1024]{1,0:T(8,128)(2,1)} %gather_fusion, pred[1024]{0:T(1024)(128)(4,1)S(1)} %get-tuple-element.17), kind=kOutput, calls=%fused_computation.4 | convolution fusion | flops 4302306304 | bytes 14697472 | tf_op jit(solution)/shard_map/dot_general | solution.py:22
  62.0 2.1 collective-permute-done
  64.1 2.8 collective-permute-start.1
  66.9 2.3 collective-permute-done.1
  69.2 2.9 collective-permute-start.2
  72.1 2.2 collective-permute-done.2
  74.3 4.3 %subtract_convert_fusion = bf16[1024,2048]{1,0:T(8,128)(2,1)S(1)} fusion(f32[1024,2048]{1,0:T(8,128)} %get-tuple-element.21, f32[1024]{0:T(1024)S(1)} %add_multiply_fusion, f32[1024]{0:T(1024)S(1)} %broadcast_divide_fusion.1, f32[2048]{0:T(1024)S(1)} %broadcast_divide_fusion), kind=kLoop, calls=%fused_computation.2 | loop fusion | flops 8388608 | bytes 12599296 | tf_op jit(solution)/shard_map/convert
  82.1 9.1 %collective-permute-done.3 = f32[512,256]{1,0:T(8,128)S(1)} collective-permute-done((f32[512,256]{1,0:T(8,128)S(1)}, f32[512,256]{1,0:T(8,128)S(1)}, u32[]{:S(2)}, u32[]{:S(2)}) %collective-permute-start.3) | collective-permute-done | bytes 524320 | tf_op jit(solution)/shard_map/ppermute | solution.py:49
  91.3 2.8 collective-permute-start.4
  94.2 5.1 %collective-permute-done.4 = f32[256,256]{1,0:T(8,128)S(1)} collective-permute-done((f32[256,256]{1,0:T(8,128)S(1)}, f32[256,256]{1,0:T(8,128)S(1)}, u32[]{:S(2)}, u32[]{:S(2)}) %collective-permute-start.4) | collective-permute-done | bytes 262176 | tf_op jit(solution)/shard_map/ppermute | solution.py:49
  99.4 3.0 collective-permute-start.5
  102.3 4.2 %collective-permute-done.5 = f32[128,256]{1,0:T(8,128)S(1)} collective-permute-done((f32[128,256]{1,0:T(8,128)S(1)}, f32[128,256]{1,0:T(8,128)S(1)}, u32[]{:S(2)}, u32[]{:S(2)}) %collective-permute-start.5) | collective-permute-done | bytes 131104 | tf_op jit(solution)/shard_map/ppermute | solution.py:49
  106.6 3.0 collective-permute-start.6
  109.6 3.6 collective-permute-done.6
  113.2 2.8 collective-permute-start.7
  116.1 5.0 %collective-permute-done.7 = f32[256,256]{1,0:T(8,128)S(1)} collective-permute-done((f32[256,256]{1,0:T(8,128)S(1)}, f32[256,256]{1,0:T(8,128)S(1)}, u32[]{:S(2)}, u32[]{:S(2)}) %collective-permute-start.7) | collective-permute-done | bytes 262176 | tf_op jit(solution)/shard_map/ppermute | solution.py:57
  123.1 7.6 %collective-permute-done.8 = f32[512,256]{1,0:T(8,128)S(1)} collective-permute-done((f32[512,256]{1,0:T(8,128)S(1)}, f32[512,256]{1,0:T(8,128)S(1)}, u32[]{:S(2)}, u32[]{:S(2)}) %collective-permute-start.8) | collective-permute-done | bytes 524320 | tf_op jit(solution)/shard_map/ppermute | solution.py:57
  130.7 3.5 fusion.5
  135.8 2.6 collective-permute-done.13
  141.1 12.8 %collective-permute-done.14 = f32[512,256]{1,0:T(8,128)S(1)} collective-permute-done((f32[512,256]{1,0:T(8,128)S(1)}, f32[512,256]{1,0:T(8,128)S(1)}, u32[]{:S(2)}, u32[]{:S(2)}) %collective-permute-start.14) | collective-permute-done | bytes 524320 | tf_op jit(solution)/shard_map/ppermute | solution.py:49
  155.2 6.3 %collective-permute-done.15 = f32[256,256]{1,0:T(8,128)S(1)} collective-permute-done((f32[256,256]{1,0:T(8,128)S(1)}, f32[256,256]{1,0:T(8,128)S(1)}, u32[]{:S(2)}, u32[]{:S(2)}) %collective-permute-start.15) | collective-permute-done | bytes 262176 | tf_op jit(solution)/shard_map/ppermute | solution.py:49
  161.6 2.1 collective-permute-start.16
  163.7 4.5 %collective-permute-done.16 = f32[128,256]{1,0:T(8,128)S(1)} collective-permute-done((f32[128,256]{1,0:T(8,128)S(1)}, f32[128,256]{1,0:T(8,128)S(1)}, u32[]{:S(2)}, u32[]{:S(2)}) %collective-permute-start.16) | collective-permute-done | bytes 131104 | tf_op jit(solution)/shard_map/ppermute | solution.py:49
  168.2 2.1 collective-permute-start.17
  170.3 3.8 collective-permute-done.17
  176.1 3.0 collective-permute-done.18
  181.1 4.4 %collective-permute-done.19 = bf16[512,256]{1,0:T(8,128)(2,1)S(1)} collective-permute-done((bf16[512,256]{1,0:T(8,128)(2,1)S(1)}, bf16[512,256]{1,0:T(8,128)(2,1)S(1)}, u32[]{:S(2)}, u32[]{:S(2)}) %collective-permute-start.19) | collective-permute-done | bytes 262176 | tf_op jit(solution)/shard_map/ppermute | solution.py:57
  190.7 12.3 %collective-permute-done.24 = f32[512,256]{1,0:T(8,128)S(1)} collective-permute-done((f32[512,256]{1,0:T(8,128)S(1)}, f32[512,256]{1,0:T(8,128)S(1)}, u32[]{:S(2)}, u32[]{:S(2)}) %collective-permute-start.24) | collective-permute-done | bytes 524320 | tf_op jit(solution)/shard_map/ppermute | solution.py:49
  203.1 3.1 collective-permute-start.25
  206.2 5.9 %collective-permute-done.25 = f32[256,256]{1,0:T(8,128)S(1)} collective-permute-done((f32[256,256]{1,0:T(8,128)S(1)}, f32[256,256]{1,0:T(8,128)S(1)}, u32[]{:S(2)}, u32[]{:S(2)}) %collective-permute-start.25) | collective-permute-done | bytes 262176 | tf_op jit(solution)/shard_map/ppermute | solution.py:49
  212.2 3.0 collective-permute-start.26
  215.2 3.6 collective-permute-done.26
  218.8 3.0 collective-permute-start.27
  222.1 3.3 collective-permute-done.27
  225.4 3.1 collective-permute-start.28
  229.3 4.3 %collective-permute-done.10 = f32[512]{0:T(512)S(1)} collective-permute-done((f32[512]{0:T(512)S(1)}, f32[512]{0:T(512)S(1)}, u32[]{:S(2)}, u32[]{:S(2)}) %collective-permute-start.10) | collective-permute-done | bytes 2080 | tf_op jit(solution)/shard_map/ppermute | solution.py:49
  237.2 2.4 collective-permute-start.12
  239.6 4.9 %collective-permute-done.21 = f32[256]{0:T(256)S(1)} collective-permute-done((f32[256]{0:T(256)S(1)}, f32[256]{0:T(256)S(1)}, u32[]{:S(2)}, u32[]{:S(2)}) %collective-permute-start.21) | collective-permute-done | bytes 1056 | tf_op jit(solution)/shard_map/ppermute | solution.py:49
  246.4 3.1 collective-permute-done.22
  249.5 2.5 collective-permute-start.23
  252.0 2.6 collective-permute-done.23
  261.2 2.3 collective-permute-done.32
  265.2 3.4 collective-permute-done.33
  270.3 2.6 collective-permute-done.34
  273.1 2.1 collective-permute-start.35
  275.2 12.2 %collective-permute-done.35 = f32[512,256]{1,0:T(8,128)S(1)} collective-permute-done((f32[512,256]{1,0:T(8,128)S(1)}, f32[512,256]{1,0:T(8,128)S(1)}, u32[]{:S(2)}, u32[]{:S(2)}) %collective-permute-start.35) | collective-permute-done | bytes 524320 | tf_op jit(solution)/shard_map/ppermute | solution.py:49
  288.6 6.7 %collective-permute-done.36 = f32[256,256]{1,0:T(8,128)S(1)} collective-permute-done((f32[256,256]{1,0:T(8,128)S(1)}, f32[256,256]{1,0:T(8,128)S(1)}, u32[]{:S(2)}, u32[]{:S(2)}) %collective-permute-start.36) | collective-permute-done | bytes 262176 | tf_op jit(solution)/shard_map/ppermute | solution.py:49
  297.0 4.9 %collective-permute-done.37 = f32[128,256]{1,0:T(8,128)S(1)} collective-permute-done((f32[128,256]{1,0:T(8,128)S(1)}, f32[128,256]{1,0:T(8,128)S(1)}, u32[]{:S(2)}, u32[]{:S(2)}) %collective-permute-start.37) | collective-permute-done | bytes 131104 | tf_op jit(solution)/shard_map/ppermute | solution.py:49
  303.6 4.5 %collective-permute-done.38 = bf16[128,256]{1,0:T(8,128)(2,1)S(1)} collective-permute-done((bf16[128,256]{1,0:T(8,128)(2,1)S(1)}, bf16[128,256]{1,0:T(8,128)(2,1)S(1)}, u32[]{:S(2)}, u32[]{:S(2)}) %collective-permute-start.38) | collective-permute-done | bytes 65568 | tf_op jit(solution)/shard_map/ppermute | solution.py:57
  309.5 3.7 collective-permute-done.39
  315.1 4.6 %collective-permute-done.40 = bf16[512,256]{1,0:T(8,128)(2,1)S(1)} collective-permute-done((bf16[512,256]{1,0:T(8,128)(2,1)S(1)}, bf16[512,256]{1,0:T(8,128)(2,1)S(1)}, u32[]{:S(2)}, u32[]{:S(2)}) %collective-permute-start.40) | collective-permute-done | bytes 262176 | tf_op jit(solution)/shard_map/ppermute | solution.py:57
  324.2 12.9 %collective-permute-done.49 = f32[512,256]{1,0:T(8,128)S(1)} collective-permute-done((f32[512,256]{1,0:T(8,128)S(1)}, f32[512,256]{1,0:T(8,128)S(1)}, u32[]{:S(2)}, u32[]{:S(2)}) %collective-permute-start.49) | collective-permute-done | bytes 524320 | tf_op jit(solution)/shard_map/ppermute | solution.py:49
  338.8 7.4 %collective-permute-done.50 = f32[256,256]{1,0:T(8,128)S(1)} collective-permute-done((f32[256,256]{1,0:T(8,128)S(1)}, f32[256,256]{1,0:T(8,128)S(1)}, u32[]{:S(2)}, u32[]{:S(2)}) %collective-permute-start.50) | collective-permute-done | bytes 262176 | tf_op jit(solution)/shard_map/ppermute | solution.py:49
  346.4 2.6 collective-permute-start.51
  348.9 4.0 %collective-permute-done.51 = f32[128,256]{1,0:T(8,128)S(1)} collective-permute-done((f32[128,256]{1,0:T(8,128)S(1)}, f32[128,256]{1,0:T(8,128)S(1)}, u32[]{:S(2)}, u32[]{:S(2)}) %collective-permute-start.51) | collective-permute-done | bytes 131104 | tf_op jit(solution)/shard_map/ppermute | solution.py:49
  353.0 2.6 collective-permute-start.52
  355.5 4.0 %collective-permute-done.52 = f32[128,256]{1,0:T(8,128)S(1)} collective-permute-done((f32[128,256]{1,0:T(8,128)S(1)}, f32[128,256]{1,0:T(8,128)S(1)}, u32[]{:S(2)}, u32[]{:S(2)}) %collective-permute-start.52) | collective-permute-done | bytes 131104 | tf_op jit(solution)/shard_map/ppermute | solution.py:57
  364.0 3.5 collective-permute-done.53
  371.2 6.7 %collective-permute-done.42 = f32[256]{0:T(256)S(1)} collective-permute-done((f32[256]{0:T(256)S(1)}, f32[256]{0:T(256)S(1)}, u32[]{:S(2)}, u32[]{:S(2)}) %collective-permute-start.42) | collective-permute-done | bytes 1056 | tf_op jit(solution)/shard_map/ppermute | solution.py:49
  377.9 3.2 collective-permute-start.43
  383.0 2.4 collective-permute-start.44
  (187 shorter events, 69.4 us)
Async XLA Ops:
  7.2 71.5 %copy-start = (bf16[2048,256]{1,0:T(8,128)(2,1)S(1)}, bf16[2048,256]{1,0:T(8,128)(2,1)}, u32[]{:S(2)}) copy-start(bf16[2048,256]{1,0:T(8,128)(2,1)} %param.13) | copy-start | bytes 3145732
  7.2 42.4 %all-gather.2.cloned.1.call-start = ((), (), s32[]{:S(2)}) async-start(), calls=%async_computation | async-start | bytes 4456448 | tf_op jit(solution)/shard_map/all_gather | solution.py:69
  14.3 8.8 %copy-start.5 = (s32[1024]{0:T(1024)S(1)}, s32[1024]{0:T(1024)}, u32[]{:S(2)}) copy-start(s32[1024]{0:T(1024)} %param.11) | copy-start | bytes 12292
  14.4 8.8 %copy-start.7 = (f32[4]{0:T(128)S(1)}, f32[4]{0:T(128)}, u32[]{:S(2)}) copy-start(f32[4]{0:T(128)} %param.12) | copy-start | bytes 52
  14.4 8.9 %copy-start.6 = (s32[2048]{0:T(1024)S(1)}, s32[2048]{0:T(1024)}, u32[]{:S(2)}) copy-start(s32[2048]{0:T(1024)} %param.8) | copy-start | bytes 24580
  60.5 3.6 collective-permute-start
  64.1 5.1 %collective-permute-start.1 = (f32[1024]{0:T(1024)S(1)}, f32[1024]{0:T(1024)S(1)}, u32[]{:S(2)}, u32[]{:S(2)}) collective-permute-start(f32[1024]{0:T(1024)S(1)} %add.298), channel_id=1, source_target_pairs={{0,16},{16,0},{32,48},{48,32},{64,80},{80,64},{96,112},{112,96},{1... | collective-permute-start | bytes 12296 | tf_op jit(solution)/shard_map/ppermute | solution.py:36
  69.2 5.1 %collective-permute-start.2 = (f32[1024]{0:T(1024)S(1)}, f32[1024]{0:T(1024)S(1)}, u32[]{:S(2)}, u32[]{:S(2)}) collective-permute-start(f32[1024]{0:T(1024)S(1)} %add.299), channel_id=1, source_target_pairs={{0,64},{16,80},{32,96},{48,112},{64,0},{80,16},{96,32},{112,48},{1... | collective-permute-start | bytes 12296 | tf_op jit(solution)/shard_map/ppermute | solution.py:36
  78.7 2.0 copy-start.2
  80.6 10.6 %collective-permute-start.3 = (f32[512,256]{1,0:T(8,128)S(1)}, f32[512,256]{1,0:T(8,128)S(1)}, u32[]{:S(2)}, u32[]{:S(2)}) collective-permute-start(f32[512,256]{1,0:T(8,128)S(1)} %constant_dynamic-slice_fusion.16), channel_id=1, source_target_pairs={{0,32},{16,48},{32,0},{48,16},{64,96},{80,112},{96,64},{112,80},{1... | collective-permute-start | bytes 1572872 | tf_op jit(solution)/shard_map/ppermute | solution.py:49
  91.3 8.0 %collective-permute-start.4 = (f32[256,256]{1,0:T(8,128)S(1)}, f32[256,256]{1,0:T(8,128)S(1)}, u32[]{:S(2)}, u32[]{:S(2)}) collective-permute-start(f32[256,256]{1,0:T(8,128)S(1)} %constant_dynamic-slice_fusion.15), channel_id=1, source_target_pairs={{0,16},{16,0},{32,48},{48,32},{64,80},{80,64},{96,112},{112,96},{1... | collective-permute-start | bytes 786440 | tf_op jit(solution)/shard_map/ppermute | solution.py:49
  99.4 7.2 %collective-permute-start.5 = (f32[128,256]{1,0:T(8,128)S(1)}, f32[128,256]{1,0:T(8,128)S(1)}, u32[]{:S(2)}, u32[]{:S(2)}) collective-permute-start(f32[128,256]{1,0:T(8,128)S(1)} %constant_dynamic-slice_fusion.14), channel_id=1, source_target_pairs={{0,64},{16,80},{32,96},{48,112},{64,0},{80,16},{96,32},{112,48},{1... | collective-permute-start | bytes 393224 | tf_op jit(solution)/shard_map/ppermute | solution.py:49
  106.6 6.6 %collective-permute-start.6 = (f32[128,256]{1,0:T(8,128)S(1)}, f32[128,256]{1,0:T(8,128)S(1)}, u32[]{:S(2)}, u32[]{:S(2)}) collective-permute-start(f32[128,256]{1,0:T(8,128)S(1)} %get-tuple-element.15), channel_id=1, source_target_pairs={{0,64},{16,80},{32,96},{48,112},{64,0},{80,16},{96,32},{112,48},{1... | collective-permute-start | bytes 393224 | tf_op jit(solution)/shard_map/ppermute | solution.py:57
  113.2 8.0 %collective-permute-start.7 = (f32[256,256]{1,0:T(8,128)S(1)}, f32[256,256]{1,0:T(8,128)S(1)}, u32[]{:S(2)}, u32[]{:S(2)}) collective-permute-start(f32[256,256]{1,0:T(8,128)S(1)} %constant_dynamic-update-slice_fusion.32), channel_id=1, source_target_pairs={{0,16},{16,0},{32,48},{48,32},{64,80},{80,64},{96,112},{112,96},{1... | collective-permute-start | bytes 786440 | tf_op jit(solution)/shard_map/ppermute | solution.py:57
  121.2 9.4 %collective-permute-start.8 = (f32[512,256]{1,0:T(8,128)S(1)}, f32[512,256]{1,0:T(8,128)S(1)}, u32[]{:S(2)}, u32[]{:S(2)}) collective-permute-start(f32[512,256]{1,0:T(8,128)S(1)} %constant_dynamic-update-slice_fusion.30), channel_id=1, source_target_pairs={{0,32},{16,48},{32,0},{48,16},{64,96},{80,112},{96,64},{112,80},{1... | collective-permute-start | bytes 1572872 | tf_op jit(solution)/shard_map/ppermute | solution.py:57
  134.2 1.4 copy-start.4
  135.6 2.7 collective-permute-start.13
  139.8 14.0 %collective-permute-start.14 = (f32[512,256]{1,0:T(8,128)S(1)}, f32[512,256]{1,0:T(8,128)S(1)}, u32[]{:S(2)}, u32[]{:S(2)}) collective-permute-start(f32[512,256]{1,0:T(8,128)S(1)} %constant_dynamic-slice_fusion.12), channel_id=1, source_target_pairs={{0,2},{1,3},{2,0},{3,1},{4,6},{5,7},{6,4},{7,5},{8,10},{9,11},{10,... | collective-permute-start | bytes 1572872 | tf_op jit(solution)/shard_map/ppermute | solution.py:49
  153.9 7.6 %collective-permute-start.15 = (f32[256,256]{1,0:T(8,128)S(1)}, f32[256,256]{1,0:T(8,128)S(1)}, u32[]{:S(2)}, u32[]{:S(2)}) collective-permute-start(f32[256,256]{1,0:T(8,128)S(1)} %constant_dynamic-slice_fusion.11), channel_id=1, source_target_pairs={{0,4},{1,5},{2,6},{3,7},{4,0},{5,1},{6,2},{7,3},{8,12},{9,13},{10,... | collective-permute-start | bytes 786440 | tf_op jit(solution)/shard_map/ppermute | solution.py:49
  161.6 6.6 %collective-permute-start.16 = (f32[128,256]{1,0:T(8,128)S(1)}, f32[128,256]{1,0:T(8,128)S(1)}, u32[]{:S(2)}, u32[]{:S(2)}) collective-permute-start(f32[128,256]{1,0:T(8,128)S(1)} %constant_dynamic-slice_fusion.10), channel_id=1, source_target_pairs={{0,8},{1,9},{2,10},{3,11},{4,12},{5,13},{6,14},{7,15},{8,0},{9,1},... | collective-permute-start | bytes 393224 | tf_op jit(solution)/shard_map/ppermute | solution.py:49
  163.7 23.9 %copy-start.3 = (bf16[1024,2048]{1,0:T(8,128)(2,1)S(1)}, bf16[1024,2048]{1,0:T(8,128)(2,1)}, u32[]{:S(2)}) copy-start(bf16[1024,2048]{1,0:T(8,128)(2,1)} %copy-done.2) | copy-start | bytes 12582916
  168.2 5.8 %collective-permute-start.17 = (bf16[128,256]{1,0:T(8,128)(2,1)S(1)}, bf16[128,256]{1,0:T(8,128)(2,1)S(1)}, u32[]{:S(2)}, u32[]{:S(2)}) collective-permute-start(bf16[128,256]{1,0:T(8,128)(2,1)S(1)} %get-tuple-element.13), channel_id=1, source_target_pairs={{0,8},{1,9},{2,10},{3,11},{4,12},{5,13},{6,14},{7,15},{8,0},{9,1},... | collective-permute-start | bytes 196616 | tf_op jit(solution)/shard_map/ppermute | solution.py:57
  174.0 5.0 %collective-permute-start.18 = (bf16[256,256]{1,0:T(8,128)(2,1)S(1)}, bf16[256,256]{1,0:T(8,128)(2,1)S(1)}, u32[]{:S(2)}, u32[]{:S(2)}) collective-permute-start(bf16[256,256]{1,0:T(8,128)(2,1)S(1)} %constant_dynamic-update-slice_fusion.26), channel_id=1, source_target_pairs={{0,4},{1,5},{2,6},{3,7},{4,0},{5,1},{6,2},{7,3},{8,12},{9,13},{10,... | collective-permute-start | bytes 393224 | tf_op jit(solution)/shard_map/ppermute | solution.py:57
  179.1 6.5 %collective-permute-start.19 = (bf16[512,256]{1,0:T(8,128)(2,1)S(1)}, bf16[512,256]{1,0:T(8,128)(2,1)S(1)}, u32[]{:S(2)}, u32[]{:S(2)}) collective-permute-start(bf16[512,256]{1,0:T(8,128)(2,1)S(1)} %constant_dynamic-update-slice_fusion.24), channel_id=1, source_target_pairs={{0,2},{1,3},{2,0},{3,1},{4,6},{5,7},{6,4},{7,5},{8,10},{9,11},{10,... | collective-permute-start | bytes 786440 | tf_op jit(solution)/shard_map/ppermute | solution.py:57
  185.6 2.0 collective-permute-start.20
  188.9 14.0 %collective-permute-start.24 = (f32[512,256]{1,0:T(8,128)S(1)}, f32[512,256]{1,0:T(8,128)S(1)}, u32[]{:S(2)}, u32[]{:S(2)}) collective-permute-start(f32[512,256]{1,0:T(8,128)S(1)} %constant_dynamic-slice_fusion.9), channel_id=1, source_target_pairs={{0,32},{16,48},{32,0},{48,16},{64,96},{80,112},{96,64},{112,80},{1... | collective-permute-start | bytes 1572872 | tf_op jit(solution)/shard_map/ppermute | solution.py:49
  203.1 9.1 %collective-permute-start.25 = (f32[256,256]{1,0:T(8,128)S(1)}, f32[256,256]{1,0:T(8,128)S(1)}, u32[]{:S(2)}, u32[]{:S(2)}) collective-permute-start(f32[256,256]{1,0:T(8,128)S(1)} %constant_dynamic-slice_fusion.8), channel_id=1, source_target_pairs={{0,16},{16,0},{32,48},{48,32},{64,80},{80,64},{96,112},{112,96},{1... | collective-permute-start | bytes 786440 | tf_op jit(solution)/shard_map/ppermute | solution.py:49
  212.2 6.6 %collective-permute-start.26 = (f32[128,256]{1,0:T(8,128)S(1)}, f32[128,256]{1,0:T(8,128)S(1)}, u32[]{:S(2)}, u32[]{:S(2)}) collective-permute-start(f32[128,256]{1,0:T(8,128)S(1)} %constant_dynamic-slice_fusion.7), channel_id=1, source_target_pairs={{0,64},{16,80},{32,96},{48,112},{64,0},{80,16},{96,32},{112,48},{1... | collective-permute-start | bytes 393224 | tf_op jit(solution)/shard_map/ppermute | solution.py:49
  218.8 6.6 %collective-permute-start.27 = (f32[128,256]{1,0:T(8,128)S(1)}, f32[128,256]{1,0:T(8,128)S(1)}, u32[]{:S(2)}, u32[]{:S(2)}) collective-permute-start(f32[128,256]{1,0:T(8,128)S(1)} %get-tuple-element.11), channel_id=1, source_target_pairs={{0,64},{16,80},{32,96},{48,112},{64,0},{80,16},{96,32},{112,48},{1... | collective-permute-start | bytes 393224 | tf_op jit(solution)/shard_map/ppermute | solution.py:57
  222.0 6.5 %collective-permute-start.9 = (f32[512]{0:T(512)S(1)}, f32[512]{0:T(512)S(1)}, u32[]{:S(2)}, u32[]{:S(2)}) collective-permute-start(f32[512]{0:T(512)S(1)} %pad_maximum_fusion), channel_id=1, source_target_pairs={{0,1},{1,0},{2,3},{3,2},{4,5},{5,4},{6,7},{7,6},{8,9},{9,8},{10,11... | collective-permute-start | bytes 6152 | tf_op jit(solution)/shard_map/ppermute | solution.py:49
  225.4 9.1 %collective-permute-start.28 = (f32[256,256]{1,0:T(8,128)S(1)}, f32[256,256]{1,0:T(8,128)S(1)}, u32[]{:S(2)}, u32[]{:S(2)}) collective-permute-start(f32[256,256]{1,0:T(8,128)S(1)} %constant_dynamic-update-slice_fusion.18), channel_id=1, source_target_pairs={{0,16},{16,0},{32,48},{48,32},{64,80},{80,64},{96,112},{112,96},{1... | collective-permute-start | bytes 786440 | tf_op jit(solution)/shard_map/ppermute | solution.py:57
  228.6 5.0 %collective-permute-start.10 = (f32[512]{0:T(512)S(1)}, f32[512]{0:T(512)S(1)}, u32[]{:S(2)}, u32[]{:S(2)}) collective-permute-start(f32[512]{0:T(512)S(1)} %fusion.12), channel_id=1, source_target_pairs={{0,2},{1,3},{2,0},{3,1},{4,6},{5,7},{6,4},{7,5},{8,10},{9,11},{10,... | collective-permute-start | bytes 6152 | tf_op jit(solution)/shard_map/ppermute | solution.py:49
  233.6 3.6 collective-permute-start.11
  234.6 20.2 %collective-permute-start.29 = (f32[512,256]{1,0:T(8,128)S(1)}, f32[512,256]{1,0:T(8,128)S(1)}, u32[]{:S(2)}, u32[]{:S(2)}) collective-permute-start(f32[512,256]{1,0:T(8,128)S(1)} %constant_dynamic-update-slice_fusion.16), channel_id=1, source_target_pairs={{0,32},{16,48},{32,0},{48,16},{64,96},{80,112},{96,64},{112,80},{1... | collective-permute-start | bytes 1572872 | tf_op jit(solution)/shard_map/ppermute | solution.py:57
  236.4 8.0 %collective-permute-start.21 = (f32[256]{0:T(256)S(1)}, f32[256]{0:T(256)S(1)}, u32[]{:S(2)}, u32[]{:S(2)}) collective-permute-start(f32[256]{0:T(256)S(1)} %multiply_reduce_fusion.1), channel_id=1, source_target_pairs={{0,32},{16,48},{32,0},{48,16},{64,96},{80,112},{96,64},{112,80},{1... | collective-permute-start | bytes 3080 | tf_op jit(solution)/shard_map/ppermute | solution.py:49
  237.2 14.8 %collective-permute-start.12 = (f32[512]{0:T(512)S(1)}, f32[512]{0:T(512)S(1)}, u32[]{:S(2)}, u32[]{:S(2)}) collective-permute-start(f32[512]{0:T(512)S(1)} %add.315), channel_id=1, source_target_pairs={{0,8},{1,9},{2,10},{3,11},{4,12},{5,13},{6,14},{7,15},{8,0},{9,1},... | collective-permute-start | bytes 6152 | tf_op jit(solution)/shard_map/ppermute | solution.py:49
  244.4 5.1 %collective-permute-start.22 = (f32[256]{0:T(256)S(1)}, f32[256]{0:T(256)S(1)}, u32[]{:S(2)}, u32[]{:S(2)}) collective-permute-start(f32[256]{0:T(256)S(1)} %add.333), channel_id=1, source_target_pairs={{0,16},{16,0},{32,48},{48,32},{64,80},{80,64},{96,112},{112,96},{1... | collective-permute-start | bytes 3080 | tf_op jit(solution)/shard_map/ppermute | solution.py:49
  249.5 5.1 %collective-permute-start.23 = (f32[256]{0:T(256)S(1)}, f32[256]{0:T(256)S(1)}, u32[]{:S(2)}, u32[]{:S(2)}) collective-permute-start(f32[256]{0:T(256)S(1)} %add.334), channel_id=1, source_target_pairs={{0,64},{16,80},{32,96},{48,112},{64,0},{80,16},{96,32},{112,48},{1... | collective-permute-start | bytes 3080 | tf_op jit(solution)/shard_map/ppermute | solution.py:49
  255.1 1.2 collective-permute-start.30
  256.4 3.6 collective-permute-start.31
  259.9 3.6 collective-permute-start.32
  263.5 5.1 %collective-permute-start.33 = (f32[256]{0:T(256)S(1)}, f32[256]{0:T(256)S(1)}, u32[]{:S(2)}, u32[]{:S(2)}) collective-permute-start(f32[256]{0:T(256)S(1)} %add.343), channel_id=1, source_target_pairs={{0,8},{1,9},{2,10},{3,11},{4,12},{5,13},{6,14},{7,15},{8,0},{9,1},... | collective-permute-start | bytes 3080 | tf_op jit(solution)/shard_map/ppermute | solution.py:36
  270.2 2.7 collective-permute-start.34
  273.1 14.3 %collective-permute-start.35 = (f32[512,256]{1,0:T(8,128)S(1)}, f32[512,256]{1,0:T(8,128)S(1)}, u32[]{:S(2)}, u32[]{:S(2)}) collective-permute-start(f32[512,256]{1,0:T(8,128)S(1)} %constant_dynamic-slice_fusion.5), channel_id=1, source_target_pairs={{0,2},{1,3},{2,0},{3,1},{4,6},{5,7},{6,4},{7,5},{8,10},{9,11},{10,... | collective-permute-start | bytes 1572872 | tf_op jit(solution)/shard_map/ppermute | solution.py:49
  287.5 7.8 %collective-permute-start.36 = (f32[256,256]{1,0:T(8,128)S(1)}, f32[256,256]{1,0:T(8,128)S(1)}, u32[]{:S(2)}, u32[]{:S(2)}) collective-permute-start(f32[256,256]{1,0:T(8,128)S(1)} %constant_dynamic-slice_fusion.4), channel_id=1, source_target_pairs={{0,4},{1,5},{2,6},{3,7},{4,0},{5,1},{6,2},{7,3},{8,12},{9,13},{10,... | collective-permute-start | bytes 786440 | tf_op jit(solution)/shard_map/ppermute | solution.py:49
  295.4 6.6 %collective-permute-start.37 = (f32[128,256]{1,0:T(8,128)S(1)}, f32[128,256]{1,0:T(8,128)S(1)}, u32[]{:S(2)}, u32[]{:S(2)}) collective-permute-start(f32[128,256]{1,0:T(8,128)S(1)} %constant_dynamic-slice_fusion.3), channel_id=1, source_target_pairs={{0,8},{1,9},{2,10},{3,11},{4,12},{5,13},{6,14},{7,15},{8,0},{9,1},... | collective-permute-start | bytes 393224 | tf_op jit(solution)/shard_map/ppermute | solution.py:49
  302.0 6.1 %collective-permute-start.38 = (bf16[128,256]{1,0:T(8,128)(2,1)S(1)}, bf16[128,256]{1,0:T(8,128)(2,1)S(1)}, u32[]{:S(2)}, u32[]{:S(2)}) collective-permute-start(bf16[128,256]{1,0:T(8,128)(2,1)S(1)} %get-tuple-element.7), channel_id=1, source_target_pairs={{0,8},{1,9},{2,10},{3,11},{4,12},{5,13},{6,14},{7,15},{8,0},{9,1},... | collective-permute-start | bytes 196616 | tf_op jit(solution)/shard_map/ppermute | solution.py:57
  308.2 5.0 %collective-permute-start.39 = (bf16[256,256]{1,0:T(8,128)(2,1)S(1)}, bf16[256,256]{1,0:T(8,128)(2,1)S(1)}, u32[]{:S(2)}, u32[]{:S(2)}) collective-permute-start(bf16[256,256]{1,0:T(8,128)(2,1)S(1)} %constant_dynamic-update-slice_fusion.12), channel_id=1, source_target_pairs={{0,4},{1,5},{2,6},{3,7},{4,0},{5,1},{6,2},{7,3},{8,12},{9,13},{10,... | collective-permute-start | bytes 393224 | tf_op jit(solution)/shard_map/ppermute | solution.py:57
  313.2 6.5 %collective-permute-start.40 = (bf16[512,256]{1,0:T(8,128)(2,1)S(1)}, bf16[512,256]{1,0:T(8,128)(2,1)S(1)}, u32[]{:S(2)}, u32[]{:S(2)}) collective-permute-start(bf16[512,256]{1,0:T(8,128)(2,1)S(1)} %constant_dynamic-update-slice_fusion.10), channel_id=1, source_target_pairs={{0,2},{1,3},{2,0},{3,1},{4,6},{5,7},{6,4},{7,5},{8,10},{9,11},{10,... | collective-permute-start | bytes 786440 | tf_op jit(solution)/shard_map/ppermute | solution.py:57
  319.7 2.0 collective-permute-start.41
  323.1 14.0 %collective-permute-start.49 = (f32[512,256]{1,0:T(8,128)S(1)}, f32[512,256]{1,0:T(8,128)S(1)}, u32[]{:S(2)}, u32[]{:S(2)}) collective-permute-start(f32[512,256]{1,0:T(8,128)S(1)} %constant_dynamic-slice_fusion.2), channel_id=1, source_target_pairs={{0,32},{16,48},{32,0},{48,16},{64,96},{80,112},{96,64},{112,80},{1... | collective-permute-start | bytes 1572872 | tf_op jit(solution)/shard_map/ppermute | solution.py:49
  337.2 9.1 %collective-permute-start.50 = (f32[256,256]{1,0:T(8,128)S(1)}, f32[256,256]{1,0:T(8,128)S(1)}, u32[]{:S(2)}, u32[]{:S(2)}) collective-permute-start(f32[256,256]{1,0:T(8,128)S(1)} %constant_dynamic-slice_fusion.1), channel_id=1, source_target_pairs={{0,16},{16,0},{32,48},{48,32},{64,80},{80,64},{96,112},{112,96},{1... | collective-permute-start | bytes 786440 | tf_op jit(solution)/shard_map/ppermute | solution.py:49
  346.4 6.6 %collective-permute-start.51 = (f32[128,256]{1,0:T(8,128)S(1)}, f32[128,256]{1,0:T(8,128)S(1)}, u32[]{:S(2)}, u32[]{:S(2)}) collective-permute-start(f32[128,256]{1,0:T(8,128)S(1)} %constant_dynamic-slice_fusion), channel_id=1, source_target_pairs={{0,64},{16,80},{32,96},{48,112},{64,0},{80,16},{96,32},{112,48},{1... | collective-permute-start | bytes 393224 | tf_op jit(solution)/shard_map/ppermute | solution.py:49
  353.0 6.6 %collective-permute-start.52 = (f32[128,256]{1,0:T(8,128)S(1)}, f32[128,256]{1,0:T(8,128)S(1)}, u32[]{:S(2)}, u32[]{:S(2)}) collective-permute-start(f32[128,256]{1,0:T(8,128)S(1)} %get-tuple-element.3), channel_id=1, source_target_pairs={{0,64},{16,80},{32,96},{48,112},{64,0},{80,16},{96,32},{112,48},{1... | collective-permute-start | bytes 393224 | tf_op jit(solution)/shard_map/ppermute | solution.py:57
  359.5 8.0 %collective-permute-start.53 = (f32[256,256]{1,0:T(8,128)S(1)}, f32[256,256]{1,0:T(8,128)S(1)}, u32[]{:S(2)}, u32[]{:S(2)}) collective-permute-start(f32[256,256]{1,0:T(8,128)S(1)} %constant_dynamic-update-slice_fusion.4), channel_id=1, source_target_pairs={{0,16},{16,0},{32,48},{48,32},{64,80},{80,64},{96,112},{112,96},{1... | collective-permute-start | bytes 786440 | tf_op jit(solution)/shard_map/ppermute | solution.py:57
  361.5 1.2 collective-permute-start.45
  362.8 7.2 %collective-permute-start.46 = (f32[256]{0:T(256)S(1)}, f32[256]{0:T(256)S(1)}, u32[]{:S(2)}, u32[]{:S(2)}) collective-permute-start(f32[256]{0:T(256)S(1)} %add.353), channel_id=1, source_target_pairs={{0,2},{1,3},{2,0},{3,1},{4,6},{5,7},{6,4},{7,5},{8,10},{9,11},{10,... | collective-permute-start | bytes 3080 | tf_op jit(solution)/shard_map/ppermute | solution.py:49
  367.5 20.7 %collective-permute-start.54 = (f32[512,256]{1,0:T(8,128)S(1)}, f32[512,256]{1,0:T(8,128)S(1)}, u32[]{:S(2)}, u32[]{:S(2)}) collective-permute-start(f32[512,256]{1,0:T(8,128)S(1)} %constant_dynamic-update-slice_fusion.2), channel_id=1, source_target_pairs={{0,32},{16,48},{32,0},{48,16},{64,96},{80,112},{96,64},{112,80},{1... | collective-permute-start | bytes 1572872 | tf_op jit(solution)/shard_map/ppermute | solution.py:57
  368.9 9.0 %collective-permute-start.42 = (f32[256]{0:T(256)S(1)}, f32[256]{0:T(256)S(1)}, u32[]{:S(2)}, u32[]{:S(2)}) collective-permute-start(f32[256]{0:T(256)S(1)} %multiply_reduce_fusion), channel_id=1, source_target_pairs={{0,32},{16,48},{32,0},{48,16},{64,96},{80,112},{96,64},{112,80},{1... | collective-permute-start | bytes 3080 | tf_op jit(solution)/shard_map/ppermute | solution.py:49
  370.0 11.1 %collective-permute-start.47 = (f32[256]{0:T(256)S(1)}, f32[256]{0:T(256)S(1)}, u32[]{:S(2)}, u32[]{:S(2)}) collective-permute-start(f32[256]{0:T(256)S(1)} %add.354), channel_id=1, source_target_pairs={{0,4},{1,5},{2,6},{3,7},{4,0},{5,1},{6,2},{7,3},{8,12},{9,13},{10,... | collective-permute-start | bytes 3080 | tf_op jit(solution)/shard_map/ppermute | solution.py:49
  377.9 5.1 %collective-permute-start.43 = (f32[256]{0:T(256)S(1)}, f32[256]{0:T(256)S(1)}, u32[]{:S(2)}, u32[]{:S(2)}) collective-permute-start(f32[256]{0:T(256)S(1)} %add.350), channel_id=1, source_target_pairs={{0,16},{16,0},{32,48},{48,32},{64,80},{80,64},{96,112},{112,96},{1... | collective-permute-start | bytes 3080 | tf_op jit(solution)/shard_map/ppermute | solution.py:49
  381.1 5.1 %collective-permute-start.48 = (f32[256]{0:T(256)S(1)}, f32[256]{0:T(256)S(1)}, u32[]{:S(2)}, u32[]{:S(2)}) collective-permute-start(f32[256]{0:T(256)S(1)} %add.355), channel_id=1, source_target_pairs={{0,8},{1,9},{2,10},{3,11},{4,12},{5,13},{6,14},{7,15},{8,0},{9,1},... | collective-permute-start | bytes 3080 | tf_op jit(solution)/shard_map/ppermute | solution.py:49
  383.0 5.1 %collective-permute-start.44 = (f32[256]{0:T(256)S(1)}, f32[256]{0:T(256)S(1)}, u32[]{:S(2)}, u32[]{:S(2)}) collective-permute-start(f32[256]{0:T(256)S(1)} %add.351), channel_id=1, source_target_pairs={{0,64},{16,80},{32,96},{48,112},{64,0},{80,16},{96,32},{112,48},{1... | collective-permute-start | bytes 3080 | tf_op jit(solution)/shard_map/ppermute | solution.py:49
  388.1 2.1 copy-start.1
Sparse Core Ops, SparseCore 0:
  9.7 39.8 all-gather.1

commit v2 on v1

--- a/solution.py
+++ b/solution.py
@@ -37,7 +37,7 @@
     return x
 
 
-def halving_sum(x, extra, axis, bits, gather_dtype):
+def halving_sum(x, extra, axis, bits, gather_dtype, wire_dtype=jnp.bfloat16):
     size = lax.axis_size(axis)
     index = lax.axis_index(axis)
     for k in bits:
@@ -46,8 +46,8 @@
         mine = (index // k) % 2
         keep = lax.dynamic_slice_in_dim(x, mine * half, half, axis=0)
         send = lax.dynamic_slice_in_dim(x, (1 - mine) * half, half, axis=0)
-        got, got_extra = lax.ppermute((send, extra), axis, perm)
-        x = keep + got
+        got, got_extra = lax.ppermute((send.astype(wire_dtype), extra), axis, perm)
+        x = keep + got.astype(jnp.float32)
         extra = extra + got_extra
     x = x.astype(gather_dtype)
     for k in reversed(bits):

time: 397 us -> 358 us (0.902)
  waiting for transfers between devices: 239 us -> 194 us
    ppermute x31, waiting for transfers between devices: 143 us -> 98.7 us  [halving_sum(): got, got_extra = lax.ppermute((send.astype(wire_dtype), extra), axis, perm)]
  transfers between devices with their start and end apart: 56 -> 56, of which waited for: 49 -> 49; matrix products, arithmetic and copies ran while one was open for 4% -> 5% of each run, Pallas kernels for 0% -> 0%
where the time goes in v2:
time: 358 us; the launch traced here: 357 us
  waiting for transfers between devices  194 us (54%)
  starting transfers between devices  95.9 us (27%)
  local copies, waits for them, and re-layouts  21.3 us (6%)
  matrix products  19.7 us (6%)
  between operations  14.8 us (4%)
  other arithmetic  11.8 us (3%)
    ppermute x31, waiting for transfers between devices, halving_sum(): got, got_extra = lax.ppermute((send.astype(wire_dtype), extra), axis, perm)  98.7 us
    ppermute x17, waiting for transfers between devices, halving_sum(): got = lax.ppermute(x, axis, perm)  53.4 us
    ppermute x31, starting transfers between devices, halving_sum(): got, got_extra = lax.ppermute((send.astype(wire_dtype), extra), axis, perm)  51 us
    ppermute x17, starting transfers between devices, halving_sum(): got = lax.ppermute(x, axis, perm)  32.5 us
    all_gather x1, waiting for transfers between devices, on_device(): gathered = lax.all_gather(summaries, 'landmark', axis=1, tiled=True)  26.2 us
    ppermute x7, waiting for transfers between devices, butterfly_sum(): x = x + lax.ppermute(x, axis, perm)  14.9 us
    ppermute x7, starting transfers between devices, butterfly_sum(): x = x + lax.ppermute(x, axis, perm)  12.3 us
    dot_general x1, matrix products, raw_block(): jnp.dot(summary_rows, anchors.T, preferred_element_type=jnp.float32)  10.9 us
  transfers between devices with their start and end apart: 56, of which 49 were waited for; matrix products, arithmetic and copies ran while one was open for 5% of the time, Pallas kernels for 0%

profile of v2, /device:TPU:0, one launch (start us, length us, event | category | flops | bytes accessed | tf_op | source)
XLA Modules:
  0.0 357.3 jit_solution(12137846888643334744)
XLA Ops:
  8.6 5.7 %gather_fusion.1 = s32[1024]{0:T(1024)S(1)} fusion(s32[2048]{0:T(1024)} %param.10, s32[1024]{0:T(1024)S(1)} %fusion.9), kind=kCustom, calls=%fused_computation.1 | custom fusion | bytes 12288 | tf_op jit(solution)/shard_map/jit(_take)/gather | solution.py:72
  14.4 8.8 %gather_fusion = bf16[1024,1024]{1,0:T(8,128)(2,1)} fusion(bf16[2048,1024]{1,0:T(8,128)(2,1)} %param.9, s32[1024]{0:T(1024)S(1)} %fusion.9), kind=kCustom, calls=%fused_computation | custom fusion | bytes 4198400 | tf_op jit(solution)/shard_map/jit(_take)/gather | solution.py:71
  23.4 26.2 %all-gather.2.cloned.1.call-done = bf16[2048,1024]{0,1:T(8,128)(2,1)} async-done(((bf16[2048,64]{0,1:T(8,128)(2,1)}), bf16[2048,1024]{0,1:T(8,128)(2,1)}) %all-gather.2.cloned.1.call-update) | async-done | bytes 4194320 | tf_op jit(solution)/shard_map/all_gather | solution.py:69
  49.6 10.9 %fusion = (f32[1024]{0:T(1024)S(1)}, f32[1024,2048]{1,0:T(8,128)}) fusion(f32[1024]{0:T(1024)S(1)} %broadcast_divide_fusion.1, f32[2048]{0:T(1024)S(1)} %broadcast_divide_fusion, bf16[2048,1024]{0,1:T(8,128)(2,1)} %all-gather.2.cloned.1.call-done, bf16[1024,1024]{1,0:T(8,128)(2,1)} %gather_fusion, pred[1024]{0:T(1024)(128)(4,1)S(1)} %get-tuple-element.17), kind=kOutput, calls=%fused_computation.4 | convolution fusion | flops 4302306304 | bytes 14697472 | tf_op jit(solution)/shard_map/dot_general | solution.py:22
  62.0 2.1 collective-permute-done
  64.1 2.8 collective-permute-start.1
  66.9 2.3 collective-permute-done.1
  69.2 2.9 collective-permute-start.2
  72.1 2.2 collective-permute-done.2
  74.3 4.3 %subtract_convert_fusion = bf16[1024,2048]{1,0:T(8,128)(2,1)S(1)} fusion(f32[1024,2048]{1,0:T(8,128)} %get-tuple-element.21, f32[1024]{0:T(1024)S(1)} %add_multiply_fusion, f32[1024]{0:T(1024)S(1)} %broadcast_divide_fusion.1, f32[2048]{0:T(1024)S(1)} %broadcast_divide_fusion), kind=kLoop, calls=%fused_computation.2 | loop fusion | flops 8388608 | bytes 12599296 | tf_op jit(solution)/shard_map/convert
  83.5 4.9 %collective-permute-done.3 = bf16[512,256]{1,0:T(8,128)(2,1)S(1)} collective-permute-done((bf16[512,256]{1,0:T(8,128)(2,1)S(1)}, bf16[512,256]{1,0:T(8,128)(2,1)S(1)}, u32[]{:S(2)}, u32[]{:S(2)}) %collective-permute-start.3) | collective-permute-done | bytes 262176 | tf_op jit(solution)/shard_map/ppermute | solution.py:49
  88.5 2.8 collective-permute-start.4
  91.3 3.7 %collective-permute-done.4 = bf16[256,256]{1,0:T(8,128)(2,1)S(1)} collective-permute-done((bf16[256,256]{1,0:T(8,128)(2,1)S(1)}, bf16[256,256]{1,0:T(8,128)(2,1)S(1)}, u32[]{:S(2)}, u32[]{:S(2)}) %collective-permute-start.4) | collective-permute-done | bytes 131104 | tf_op jit(solution)/shard_map/ppermute | solution.py:49
  95.1 3.0 collective-permute-start.5
  98.0 2.9 collective-permute-done.5
  101.0 3.0 collective-permute-start.6
  104.0 3.6 %collective-permute-done.6 = f32[128,256]{1,0:T(8,128)S(1)} collective-permute-done((f32[128,256]{1,0:T(8,128)S(1)}, f32[128,256]{1,0:T(8,128)S(1)}, u32[]{:S(2)}, u32[]{:S(2)}) %collective-permute-start.6) | collective-permute-done | bytes 131104 | tf_op jit(solution)/shard_map/ppermute | solution.py:57
  107.5 2.8 collective-permute-start.7
  110.5 5.0 %collective-permute-done.7 = f32[256,256]{1,0:T(8,128)S(1)} collective-permute-done((f32[256,256]{1,0:T(8,128)S(1)}, f32[256,256]{1,0:T(8,128)S(1)}, u32[]{:S(2)}, u32[]{:S(2)}) %collective-permute-start.7) | collective-permute-done | bytes 262176 | tf_op jit(solution)/shard_map/ppermute | solution.py:57
  117.4 7.5 %collective-permute-done.8 = f32[512,256]{1,0:T(8,128)S(1)} collective-permute-done((f32[512,256]{1,0:T(8,128)S(1)}, f32[512,256]{1,0:T(8,128)S(1)}, u32[]{:S(2)}, u32[]{:S(2)}) %collective-permute-start.8) | collective-permute-done | bytes 524320 | tf_op jit(solution)/shard_map/ppermute | solution.py:57
  125.0 3.5 fusion.5
  135.5 7.3 %collective-permute-done.14 = bf16[512,256]{1,0:T(8,128)(2,1)S(1)} collective-permute-done((bf16[512,256]{1,0:T(8,128)(2,1)}, bf16[512,256]{1,0:T(8,128)(2,1)S(1)}, u32[]{:S(2)}, u32[]{:S(2)}) %collective-permute-start.14) | collective-permute-done | bytes 262176 | tf_op jit(solution)/shard_map/ppermute | solution.py:49
  145.0 3.8 %collective-permute-done.15 = bf16[256,256]{1,0:T(8,128)(2,1)S(1)} collective-permute-done((bf16[256,256]{1,0:T(8,128)(2,1)S(1)}, bf16[256,256]{1,0:T(8,128)(2,1)S(1)}, u32[]{:S(2)}, u32[]{:S(2)}) %collective-permute-start.15) | collective-permute-done | bytes 131104 | tf_op jit(solution)/shard_map/ppermute | solution.py:49
  149.8 2.1 collective-permute-start.16
  151.9 3.8 %collective-permute-done.16 = bf16[128,256]{1,0:T(8,128)(2,1)S(1)} collective-permute-done((bf16[128,256]{1,0:T(8,128)(2,1)S(1)}, bf16[128,256]{1,0:T(8,128)(2,1)S(1)}, u32[]{:S(2)}, u32[]{:S(2)}) %collective-permute-start.16) | collective-permute-done | bytes 65568 | tf_op jit(solution)/shard_map/ppermute | solution.py:49
  155.7 2.1 collective-permute-start.17
  157.8 4.0 %collective-permute-done.17 = bf16[128,256]{1,0:T(8,128)(2,1)S(1)} collective-permute-done((bf16[128,256]{1,0:T(8,128)(2,1)S(1)}, bf16[128,256]{1,0:T(8,128)(2,1)S(1)}, u32[]{:S(2)}, u32[]{:S(2)}) %collective-permute-start.17) | collective-permute-done | bytes 65568 | tf_op jit(solution)/shard_map/ppermute | solution.py:57
  163.6 3.2 collective-permute-done.18
  168.7 4.6 %collective-permute-done.19 = bf16[512,256]{1,0:T(8,128)(2,1)S(1)} collective-permute-done((bf16[512,256]{1,0:T(8,128)(2,1)S(1)}, bf16[512,256]{1,0:T(8,128)(2,1)S(1)}, u32[]{:S(2)}, u32[]{:S(2)}) %collective-permute-start.19) | collective-permute-done | bytes 262176 | tf_op jit(solution)/shard_map/ppermute | solution.py:57
  178.5 6.6 %collective-permute-done.24 = bf16[512,256]{1,0:T(8,128)(2,1)S(1)} collective-permute-done((bf16[512,256]{1,0:T(8,128)(2,1)S(1)}, bf16[512,256]{1,0:T(8,128)(2,1)S(1)}, u32[]{:S(2)}, u32[]{:S(2)}) %collective-permute-start.24) | collective-permute-done | bytes 262176 | tf_op jit(solution)/shard_map/ppermute | solution.py:49
  185.2 3.2 collective-permute-start.25
  188.4 3.3 collective-permute-done.25
  191.8 3.0 collective-permute-start.26
  194.8 2.9 collective-permute-done.26
  197.7 3.0 collective-permute-start.27
  200.9 3.3 collective-permute-done.27
  204.3 3.2 collective-permute-start.28
  208.2 4.3 %collective-permute-done.10 = f32[512]{0:T(512)S(1)} collective-permute-done((f32[512]{0:T(512)S(1)}, f32[512]{0:T(512)S(1)}, u32[]{:S(2)}, u32[]{:S(2)}) %collective-permute-start.10) | collective-permute-done | bytes 2080 | tf_op jit(solution)/shard_map/ppermute | solution.py:49
  216.1 2.1 collective-permute-start.12
  218.2 5.0 %collective-permute-done.21 = f32[256]{0:T(256)S(1)} collective-permute-done((f32[256]{0:T(256)S(1)}, f32[256]{0:T(256)S(1)}, u32[]{:S(2)}, u32[]{:S(2)}) %collective-permute-start.21) | collective-permute-done | bytes 1056 | tf_op jit(solution)/shard_map/ppermute | solution.py:49
  225.3 3.1 collective-permute-done.22
  228.3 2.5 collective-permute-start.23
  230.8 2.6 collective-permute-done.23
  240.0 2.4 collective-permute-done.32
  244.4 3.0 collective-permute-done.33
  253.0 6.6 %collective-permute-done.35 = bf16[512,256]{1,0:T(8,128)(2,1)S(1)} collective-permute-done((bf16[512,256]{1,0:T(8,128)(2,1)S(1)}, bf16[512,256]{1,0:T(8,128)(2,1)S(1)}, u32[]{:S(2)}, u32[]{:S(2)}) %collective-permute-start.35) | collective-permute-done | bytes 262176 | tf_op jit(solution)/shard_map/ppermute | solution.py:49
  260.9 3.9 %collective-permute-done.36 = bf16[256,256]{1,0:T(8,128)(2,1)S(1)} collective-permute-done((bf16[256,256]{1,0:T(8,128)(2,1)S(1)}, bf16[256,256]{1,0:T(8,128)(2,1)S(1)}, u32[]{:S(2)}, u32[]{:S(2)}) %collective-permute-start.36) | collective-permute-done | bytes 131104 | tf_op jit(solution)/shard_map/ppermute | solution.py:49
  264.8 2.3 collective-permute-start.37
  267.1 3.6 collective-permute-done.37
  270.7 2.3 collective-permute-start.38
  273.0 3.9 %collective-permute-done.38 = bf16[128,256]{1,0:T(8,128)(2,1)S(1)} collective-permute-done((bf16[128,256]{1,0:T(8,128)(2,1)S(1)}, bf16[128,256]{1,0:T(8,128)(2,1)S(1)}, u32[]{:S(2)}, u32[]{:S(2)}) %collective-permute-start.38) | collective-permute-done | bytes 65568 | tf_op jit(solution)/shard_map/ppermute | solution.py:57
  278.5 3.4 collective-permute-done.39
  282.0 2.1 collective-permute-start.40
  284.2 4.3 %collective-permute-done.40 = bf16[512,256]{1,0:T(8,128)(2,1)S(1)} collective-permute-done((bf16[512,256]{1,0:T(8,128)(2,1)S(1)}, bf16[512,256]{1,0:T(8,128)(2,1)S(1)}, u32[]{:S(2)}, u32[]{:S(2)}) %collective-permute-start.40) | collective-permute-done | bytes 262176 | tf_op jit(solution)/shard_map/ppermute | solution.py:57
  292.9 7.4 %collective-permute-done.49 = bf16[512,256]{1,0:T(8,128)(2,1)S(1)} collective-permute-done((bf16[512,256]{1,0:T(8,128)(2,1)S(1)}, bf16[512,256]{1,0:T(8,128)(2,1)S(1)}, u32[]{:S(2)}, u32[]{:S(2)}) %collective-permute-start.49) | collective-permute-done | bytes 262176 | tf_op jit(solution)/shard_map/ppermute | solution.py:49
  302.2 4.7 %collective-permute-done.50 = bf16[256,256]{1,0:T(8,128)(2,1)S(1)} collective-permute-done((bf16[256,256]{1,0:T(8,128)(2,1)S(1)}, bf16[256,256]{1,0:T(8,128)(2,1)S(1)}, u32[]{:S(2)}, u32[]{:S(2)}) %collective-permute-start.50) | collective-permute-done | bytes 131104 | tf_op jit(solution)/shard_map/ppermute | solution.py:49
  307.0 2.6 collective-permute-start.51
  309.5 3.3 collective-permute-done.51
  312.9 2.6 collective-permute-start.52
  315.4 4.0 %collective-permute-done.52 = f32[128,256]{1,0:T(8,128)S(1)} collective-permute-done((f32[128,256]{1,0:T(8,128)S(1)}, f32[128,256]{1,0:T(8,128)S(1)}, u32[]{:S(2)}, u32[]{:S(2)}) %collective-permute-start.52) | collective-permute-done | bytes 131104 | tf_op jit(solution)/shard_map/ppermute | solution.py:57
  324.3 3.1 collective-permute-done.53
  331.4 6.9 %collective-permute-done.42 = f32[256]{0:T(256)S(1)} collective-permute-done((f32[256]{0:T(256)S(1)}, f32[256]{0:T(256)S(1)}, u32[]{:S(2)}, u32[]{:S(2)}) %collective-permute-start.42) | collective-permute-done | bytes 1056 | tf_op jit(solution)/shard_map/ppermute | solution.py:49
  338.3 3.0 collective-permute-start.43
  343.3 2.3 collective-permute-start.44
  (187 shorter events, 75.2 us)
Async XLA Ops:
  7.2 73.5 %copy-start = (bf16[2048,256]{1,0:T(8,128)(2,1)S(1)}, bf16[2048,256]{1,0:T(8,128)(2,1)}, u32[]{:S(2)}) copy-start(bf16[2048,256]{1,0:T(8,128)(2,1)} %param.13) | copy-start | bytes 3145732
  7.2 42.4 %all-gather.2.cloned.1.call-start = ((), (), s32[]{:S(2)}) async-start(), calls=%async_computation | async-start | bytes 4456448 | tf_op jit(solution)/shard_map/all_gather | solution.py:69
  14.3 8.8 %copy-start.5 = (s32[1024]{0:T(1024)S(1)}, s32[1024]{0:T(1024)}, u32[]{:S(2)}) copy-start(s32[1024]{0:T(1024)} %param.11) | copy-start | bytes 12292
  14.4 8.8 %copy-start.7 = (f32[4]{0:T(128)S(1)}, f32[4]{0:T(128)}, u32[]{:S(2)}) copy-start(f32[4]{0:T(128)} %param.12) | copy-start | bytes 52
  14.4 8.9 %copy-start.6 = (s32[2048]{0:T(1024)S(1)}, s32[2048]{0:T(1024)}, u32[]{:S(2)}) copy-start(s32[2048]{0:T(1024)} %param.8) | copy-start | bytes 24580
  60.5 3.6 %collective-permute-start = (f32[1024]{0:T(1024)S(1)}, f32[1024]{0:T(1024)S(1)}, u32[]{:S(2)}, u32[]{:S(2)}) collective-permute-start(f32[1024]{0:T(1024)S(1)} %get-tuple-element.20), channel_id=1, source_target_pairs={{0,32},{16,48},{32,0},{48,16},{64,96},{80,112},{96,64},{112,80},{1... | collective-permute-start | bytes 12296 | tf_op jit(solution)/shard_map/ppermute | solution.py:36
  64.1 5.1 %collective-permute-start.1 = (f32[1024]{0:T(1024)S(1)}, f32[1024]{0:T(1024)S(1)}, u32[]{:S(2)}, u32[]{:S(2)}) collective-permute-start(f32[1024]{0:T(1024)S(1)} %add.298), channel_id=1, source_target_pairs={{0,16},{16,0},{32,48},{48,32},{64,80},{80,64},{96,112},{112,96},{1... | collective-permute-start | bytes 12296 | tf_op jit(solution)/shard_map/ppermute | solution.py:36
  69.2 5.1 %collective-permute-start.2 = (f32[1024]{0:T(1024)S(1)}, f32[1024]{0:T(1024)S(1)}, u32[]{:S(2)}, u32[]{:S(2)}) collective-permute-start(f32[1024]{0:T(1024)S(1)} %add.299), channel_id=1, source_target_pairs={{0,64},{16,80},{32,96},{48,112},{64,0},{80,16},{96,32},{112,48},{1... | collective-permute-start | bytes 12296 | tf_op jit(solution)/shard_map/ppermute | solution.py:36
  78.7 2.0 copy-start.1
  81.9 6.5 %collective-permute-start.3 = (bf16[512,256]{1,0:T(8,128)(2,1)S(1)}, bf16[512,256]{1,0:T(8,128)(2,1)S(1)}, u32[]{:S(2)}, u32[]{:S(2)}) collective-permute-start(bf16[512,256]{1,0:T(8,128)(2,1)S(1)} %dynamic-slice_convert_fusion.6), channel_id=1, source_target_pairs={{0,32},{16,48},{32,0},{48,16},{64,96},{80,112},{96,64},{112,80},{1... | collective-permute-start | bytes 786440 | tf_op jit(solution)/shard_map/ppermute | solution.py:49
  88.5 6.6 %collective-permute-start.4 = (bf16[256,256]{1,0:T(8,128)(2,1)S(1)}, bf16[256,256]{1,0:T(8,128)(2,1)S(1)}, u32[]{:S(2)}, u32[]{:S(2)}) collective-permute-start(bf16[256,256]{1,0:T(8,128)(2,1)S(1)} %dynamic-slice_convert_fusion.11), channel_id=1, source_target_pairs={{0,16},{16,0},{32,48},{48,32},{64,80},{80,64},{96,112},{112,96},{1... | collective-permute-start | bytes 393224 | tf_op jit(solution)/shard_map/ppermute | solution.py:49
  95.1 5.8 %collective-permute-start.5 = (bf16[128,256]{1,0:T(8,128)(2,1)S(1)}, bf16[128,256]{1,0:T(8,128)(2,1)S(1)}, u32[]{:S(2)}, u32[]{:S(2)}) collective-permute-start(bf16[128,256]{1,0:T(8,128)(2,1)S(1)} %dynamic-slice_convert_fusion.16), channel_id=1, source_target_pairs={{0,64},{16,80},{32,96},{48,112},{64,0},{80,16},{96,32},{112,48},{1... | collective-permute-start | bytes 196616 | tf_op jit(solution)/shard_map/ppermute | solution.py:49
  101.0 6.6 %collective-permute-start.6 = (f32[128,256]{1,0:T(8,128)S(1)}, f32[128,256]{1,0:T(8,128)S(1)}, u32[]{:S(2)}, u32[]{:S(2)}) collective-permute-start(f32[128,256]{1,0:T(8,128)S(1)} %get-tuple-element.15), channel_id=1, source_target_pairs={{0,64},{16,80},{32,96},{48,112},{64,0},{80,16},{96,32},{112,48},{1... | collective-permute-start | bytes 393224 | tf_op jit(solution)/shard_map/ppermute | solution.py:57
  107.5 8.0 %collective-permute-start.7 = (f32[256,256]{1,0:T(8,128)S(1)}, f32[256,256]{1,0:T(8,128)S(1)}, u32[]{:S(2)}, u32[]{:S(2)}) collective-permute-start(f32[256,256]{1,0:T(8,128)S(1)} %constant_dynamic-update-slice_fusion.32), channel_id=1, source_target_pairs={{0,16},{16,0},{32,48},{48,32},{64,80},{80,64},{96,112},{112,96},{1... | collective-permute-start | bytes 786440 | tf_op jit(solution)/shard_map/ppermute | solution.py:57
  115.5 9.4 %collective-permute-start.8 = (f32[512,256]{1,0:T(8,128)S(1)}, f32[512,256]{1,0:T(8,128)S(1)}, u32[]{:S(2)}, u32[]{:S(2)}) collective-permute-start(f32[512,256]{1,0:T(8,128)S(1)} %constant_dynamic-update-slice_fusion.30), channel_id=1, source_target_pairs={{0,32},{16,48},{32,0},{48,16},{64,96},{80,112},{96,64},{112,80},{1... | collective-permute-start | bytes 1572872 | tf_op jit(solution)/shard_map/ppermute | solution.py:57
  128.6 1.4 copy-start.4
  130.0 2.1 collective-permute-start.13
  134.3 8.6 %collective-permute-start.14 = (bf16[512,256]{1,0:T(8,128)(2,1)}, bf16[512,256]{1,0:T(8,128)(2,1)S(1)}, u32[]{:S(2)}, u32[]{:S(2)}) collective-permute-start(bf16[512,256]{1,0:T(8,128)(2,1)} %dynamic-slice_convert_fusion.5), channel_id=1, source_target_pairs={{0,2},{1,3},{2,0},{3,1},{4,6},{5,7},{6,4},{7,5},{8,10},{9,11},{10,... | collective-permute-start | bytes 786440 | tf_op jit(solution)/shard_map/ppermute | solution.py:49
  142.9 0.8 copy-start.3
  143.8 5.0 %collective-permute-start.15 = (bf16[256,256]{1,0:T(8,128)(2,1)S(1)}, bf16[256,256]{1,0:T(8,128)(2,1)S(1)}, u32[]{:S(2)}, u32[]{:S(2)}) collective-permute-start(bf16[256,256]{1,0:T(8,128)(2,1)S(1)} %dynamic-slice_convert_fusion.10), channel_id=1, source_target_pairs={{0,4},{1,5},{2,6},{3,7},{4,0},{5,1},{6,2},{7,3},{8,12},{9,13},{10,... | collective-permute-start | bytes 393224 | tf_op jit(solution)/shard_map/ppermute | solution.py:49
  149.8 5.8 %collective-permute-start.16 = (bf16[128,256]{1,0:T(8,128)(2,1)S(1)}, bf16[128,256]{1,0:T(8,128)(2,1)S(1)}, u32[]{:S(2)}, u32[]{:S(2)}) collective-permute-start(bf16[128,256]{1,0:T(8,128)(2,1)S(1)} %dynamic-slice_convert_fusion.15), channel_id=1, source_target_pairs={{0,8},{1,9},{2,10},{3,11},{4,12},{5,13},{6,14},{7,15},{8,0},{9,1},... | collective-permute-start | bytes 196616 | tf_op jit(solution)/shard_map/ppermute | solution.py:49
  151.9 23.5 %copy-start.2 = (bf16[1024,2048]{1,0:T(8,128)(2,1)S(1)}, bf16[1024,2048]{1,0:T(8,128)(2,1)}, u32[]{:S(2)}) copy-start(bf16[1024,2048]{1,0:T(8,128)(2,1)} %copy-done.1) | copy-start | bytes 12582916
  155.7 6.1 %collective-permute-start.17 = (bf16[128,256]{1,0:T(8,128)(2,1)S(1)}, bf16[128,256]{1,0:T(8,128)(2,1)S(1)}, u32[]{:S(2)}, u32[]{:S(2)}) collective-permute-start(bf16[128,256]{1,0:T(8,128)(2,1)S(1)} %get-tuple-element.13), channel_id=1, source_target_pairs={{0,8},{1,9},{2,10},{3,11},{4,12},{5,13},{6,14},{7,15},{8,0},{9,1},... | collective-permute-start | bytes 196616 | tf_op jit(solution)/shard_map/ppermute | solution.py:57
  161.8 5.0 %collective-permute-start.18 = (bf16[256,256]{1,0:T(8,128)(2,1)S(1)}, bf16[256,256]{1,0:T(8,128)(2,1)S(1)}, u32[]{:S(2)}, u32[]{:S(2)}) collective-permute-start(bf16[256,256]{1,0:T(8,128)(2,1)S(1)} %constant_dynamic-update-slice_fusion.26), channel_id=1, source_target_pairs={{0,4},{1,5},{2,6},{3,7},{4,0},{5,1},{6,2},{7,3},{8,12},{9,13},{10,... | collective-permute-start | bytes 393224 | tf_op jit(solution)/shard_map/ppermute | solution.py:57
  166.8 6.5 %collective-permute-start.19 = (bf16[512,256]{1,0:T(8,128)(2,1)S(1)}, bf16[512,256]{1,0:T(8,128)(2,1)S(1)}, u32[]{:S(2)}, u32[]{:S(2)}) collective-permute-start(bf16[512,256]{1,0:T(8,128)(2,1)S(1)} %constant_dynamic-update-slice_fusion.24), channel_id=1, source_target_pairs={{0,2},{1,3},{2,0},{3,1},{4,6},{5,7},{6,4},{7,5},{8,10},{9,11},{10,... | collective-permute-start | bytes 786440 | tf_op jit(solution)/shard_map/ppermute | solution.py:57
  173.3 2.0 collective-permute-start.20
  176.7 8.4 %collective-permute-start.24 = (bf16[512,256]{1,0:T(8,128)(2,1)S(1)}, bf16[512,256]{1,0:T(8,128)(2,1)S(1)}, u32[]{:S(2)}, u32[]{:S(2)}) collective-permute-start(bf16[512,256]{1,0:T(8,128)(2,1)S(1)} %dynamic-slice_convert_fusion.4), channel_id=1, source_target_pairs={{0,32},{16,48},{32,0},{48,16},{64,96},{80,112},{96,64},{112,80},{1... | collective-permute-start | bytes 786440 | tf_op jit(solution)/shard_map/ppermute | solution.py:49
  185.2 6.6 %collective-permute-start.25 = (bf16[256,256]{1,0:T(8,128)(2,1)S(1)}, bf16[256,256]{1,0:T(8,128)(2,1)S(1)}, u32[]{:S(2)}, u32[]{:S(2)}) collective-permute-start(bf16[256,256]{1,0:T(8,128)(2,1)S(1)} %dynamic-slice_convert_fusion.9), channel_id=1, source_target_pairs={{0,16},{16,0},{32,48},{48,32},{64,80},{80,64},{96,112},{112,96},{1... | collective-permute-start | bytes 393224 | tf_op jit(solution)/shard_map/ppermute | solution.py:49
  191.8 5.8 %collective-permute-start.26 = (bf16[128,256]{1,0:T(8,128)(2,1)S(1)}, bf16[128,256]{1,0:T(8,128)(2,1)S(1)}, u32[]{:S(2)}, u32[]{:S(2)}) collective-permute-start(bf16[128,256]{1,0:T(8,128)(2,1)S(1)} %dynamic-slice_convert_fusion.14), channel_id=1, source_target_pairs={{0,64},{16,80},{32,96},{48,112},{64,0},{80,16},{96,32},{112,48},{1... | collective-permute-start | bytes 196616 | tf_op jit(solution)/shard_map/ppermute | solution.py:49
  197.7 6.6 %collective-permute-start.27 = (f32[128,256]{1,0:T(8,128)S(1)}, f32[128,256]{1,0:T(8,128)S(1)}, u32[]{:S(2)}, u32[]{:S(2)}) collective-permute-start(f32[128,256]{1,0:T(8,128)S(1)} %get-tuple-element.11), channel_id=1, source_target_pairs={{0,64},{16,80},{32,96},{48,112},{64,0},{80,16},{96,32},{112,48},{1... | collective-permute-start | bytes 393224 | tf_op jit(solution)/shard_map/ppermute | solution.py:57
  200.8 6.6 %collective-permute-start.9 = (f32[512]{0:T(512)S(1)}, f32[512]{0:T(512)S(1)}, u32[]{:S(2)}, u32[]{:S(2)}) collective-permute-start(f32[512]{0:T(512)S(1)} %pad_maximum_fusion), channel_id=1, source_target_pairs={{0,1},{1,0},{2,3},{3,2},{4,5},{5,4},{6,7},{7,6},{8,9},{9,8},{10,11... | collective-permute-start | bytes 6152 | tf_op jit(solution)/shard_map/ppermute | solution.py:49
  204.3 9.1 %collective-permute-start.28 = (f32[256,256]{1,0:T(8,128)S(1)}, f32[256,256]{1,0:T(8,128)S(1)}, u32[]{:S(2)}, u32[]{:S(2)}) collective-permute-start(f32[256,256]{1,0:T(8,128)S(1)} %constant_dynamic-update-slice_fusion.18), channel_id=1, source_target_pairs={{0,16},{16,0},{32,48},{48,32},{64,80},{80,64},{96,112},{112,96},{1... | collective-permute-start | bytes 786440 | tf_op jit(solution)/shard_map/ppermute | solution.py:57
  207.5 5.0 %collective-permute-start.10 = (f32[512]{0:T(512)S(1)}, f32[512]{0:T(512)S(1)}, u32[]{:S(2)}, u32[]{:S(2)}) collective-permute-start(f32[512]{0:T(512)S(1)} %fusion.12), channel_id=1, source_target_pairs={{0,2},{1,3},{2,0},{3,1},{4,6},{5,7},{6,4},{7,5},{8,10},{9,11},{10,... | collective-permute-start | bytes 6152 | tf_op jit(solution)/shard_map/ppermute | solution.py:49
  212.5 3.6 %collective-permute-start.11 = (f32[512]{0:T(512)S(1)}, f32[512]{0:T(512)S(1)}, u32[]{:S(2)}, u32[]{:S(2)}) collective-permute-start(f32[512]{0:T(512)S(1)} %add.314), channel_id=1, source_target_pairs={{0,4},{1,5},{2,6},{3,7},{4,0},{5,1},{6,2},{7,3},{8,12},{9,13},{10,... | collective-permute-start | bytes 6152 | tf_op jit(solution)/shard_map/ppermute | solution.py:49
  213.4 20.1 %collective-permute-start.29 = (f32[512,256]{1,0:T(8,128)S(1)}, f32[512,256]{1,0:T(8,128)S(1)}, u32[]{:S(2)}, u32[]{:S(2)}) collective-permute-start(f32[512,256]{1,0:T(8,128)S(1)} %constant_dynamic-update-slice_fusion.16), channel_id=1, source_target_pairs={{0,32},{16,48},{32,0},{48,16},{64,96},{80,112},{96,64},{112,80},{1... | collective-permute-start | bytes 1572872 | tf_op jit(solution)/shard_map/ppermute | solution.py:57
  215.3 8.0 %collective-permute-start.21 = (f32[256]{0:T(256)S(1)}, f32[256]{0:T(256)S(1)}, u32[]{:S(2)}, u32[]{:S(2)}) collective-permute-start(f32[256]{0:T(256)S(1)} %multiply_reduce_fusion.1), channel_id=1, source_target_pairs={{0,32},{16,48},{32,0},{48,16},{64,96},{80,112},{96,64},{112,80},{1... | collective-permute-start | bytes 3080 | tf_op jit(solution)/shard_map/ppermute | solution.py:49
  216.1 14.7 %collective-permute-start.12 = (f32[512]{0:T(512)S(1)}, f32[512]{0:T(512)S(1)}, u32[]{:S(2)}, u32[]{:S(2)}) collective-permute-start(f32[512]{0:T(512)S(1)} %add.315), channel_id=1, source_target_pairs={{0,8},{1,9},{2,10},{3,11},{4,12},{5,13},{6,14},{7,15},{8,0},{9,1},... | collective-permute-start | bytes 6152 | tf_op jit(solution)/shard_map/ppermute | solution.py:49
  223.2 5.1 %collective-permute-start.22 = (f32[256]{0:T(256)S(1)}, f32[256]{0:T(256)S(1)}, u32[]{:S(2)}, u32[]{:S(2)}) collective-permute-start(f32[256]{0:T(256)S(1)} %add.333), channel_id=1, source_target_pairs={{0,16},{16,0},{32,48},{48,32},{64,80},{80,64},{96,112},{112,96},{1... | collective-permute-start | bytes 3080 | tf_op jit(solution)/shard_map/ppermute | solution.py:49
  228.3 5.1 %collective-permute-start.23 = (f32[256]{0:T(256)S(1)}, f32[256]{0:T(256)S(1)}, u32[]{:S(2)}, u32[]{:S(2)}) collective-permute-start(f32[256]{0:T(256)S(1)} %add.334), channel_id=1, source_target_pairs={{0,64},{16,80},{32,96},{48,112},{64,0},{80,16},{96,32},{112,48},{1... | collective-permute-start | bytes 3080 | tf_op jit(solution)/shard_map/ppermute | solution.py:49
  233.9 1.2 collective-permute-start.30
  235.2 3.6 %collective-permute-start.31 = (f32[256]{0:T(256)S(1)}, f32[256]{0:T(256)S(1)}, u32[]{:S(2)}, u32[]{:S(2)}) collective-permute-start(f32[256]{0:T(256)S(1)} %add.341), channel_id=1, source_target_pairs={{0,2},{1,3},{2,0},{3,1},{4,6},{5,7},{6,4},{7,5},{8,10},{9,11},{10,... | collective-permute-start | bytes 3080 | tf_op jit(solution)/shard_map/ppermute | solution.py:36
  238.7 3.6 %collective-permute-start.32 = (f32[256]{0:T(256)S(1)}, f32[256]{0:T(256)S(1)}, u32[]{:S(2)}, u32[]{:S(2)}) collective-permute-start(f32[256]{0:T(256)S(1)} %add.342), channel_id=1, source_target_pairs={{0,4},{1,5},{2,6},{3,7},{4,0},{5,1},{6,2},{7,3},{8,12},{9,13},{10,... | collective-permute-start | bytes 3080 | tf_op jit(solution)/shard_map/ppermute | solution.py:36
  242.3 5.1 %collective-permute-start.33 = (f32[256]{0:T(256)S(1)}, f32[256]{0:T(256)S(1)}, u32[]{:S(2)}, u32[]{:S(2)}) collective-permute-start(f32[256]{0:T(256)S(1)} %add.343), channel_id=1, source_target_pairs={{0,8},{1,9},{2,10},{3,11},{4,12},{5,13},{6,14},{7,15},{8,0},{9,1},... | collective-permute-start | bytes 3080 | tf_op jit(solution)/shard_map/ppermute | solution.py:36
  249.0 2.0 collective-permute-start.34
  251.1 8.5 %collective-permute-start.35 = (bf16[512,256]{1,0:T(8,128)(2,1)S(1)}, bf16[512,256]{1,0:T(8,128)(2,1)S(1)}, u32[]{:S(2)}, u32[]{:S(2)}) collective-permute-start(bf16[512,256]{1,0:T(8,128)(2,1)S(1)} %dynamic-slice_convert_fusion.3), channel_id=1, source_target_pairs={{0,2},{1,3},{2,0},{3,1},{4,6},{5,7},{6,4},{7,5},{8,10},{9,11},{10,... | collective-permute-start | bytes 786440 | tf_op jit(solution)/shard_map/ppermute | solution.py:49
  259.7 5.0 %collective-permute-start.36 = (bf16[256,256]{1,0:T(8,128)(2,1)S(1)}, bf16[256,256]{1,0:T(8,128)(2,1)S(1)}, u32[]{:S(2)}, u32[]{:S(2)}) collective-permute-start(bf16[256,256]{1,0:T(8,128)(2,1)S(1)} %dynamic-slice_convert_fusion.8), channel_id=1, source_target_pairs={{0,4},{1,5},{2,6},{3,7},{4,0},{5,1},{6,2},{7,3},{8,12},{9,13},{10,... | collective-permute-start | bytes 393224 | tf_op jit(solution)/shard_map/ppermute | solution.py:49
  264.8 5.8 %collective-permute-start.37 = (bf16[128,256]{1,0:T(8,128)(2,1)S(1)}, bf16[128,256]{1,0:T(8,128)(2,1)S(1)}, u32[]{:S(2)}, u32[]{:S(2)}) collective-permute-start(bf16[128,256]{1,0:T(8,128)(2,1)S(1)} %dynamic-slice_convert_fusion.13), channel_id=1, source_target_pairs={{0,8},{1,9},{2,10},{3,11},{4,12},{5,13},{6,14},{7,15},{8,0},{9,1},... | collective-permute-start | bytes 196616 | tf_op jit(solution)/shard_map/ppermute | solution.py:49
  270.7 6.2 %collective-permute-start.38 = (bf16[128,256]{1,0:T(8,128)(2,1)S(1)}, bf16[128,256]{1,0:T(8,128)(2,1)S(1)}, u32[]{:S(2)}, u32[]{:S(2)}) collective-permute-start(bf16[128,256]{1,0:T(8,128)(2,1)S(1)} %get-tuple-element.7), channel_id=1, source_target_pairs={{0,8},{1,9},{2,10},{3,11},{4,12},{5,13},{6,14},{7,15},{8,0},{9,1},... | collective-permute-start | bytes 196616 | tf_op jit(solution)/shard_map/ppermute | solution.py:57
  276.9 5.0 %collective-permute-start.39 = (bf16[256,256]{1,0:T(8,128)(2,1)S(1)}, bf16[256,256]{1,0:T(8,128)(2,1)S(1)}, u32[]{:S(2)}, u32[]{:S(2)}) collective-permute-start(bf16[256,256]{1,0:T(8,128)(2,1)S(1)} %constant_dynamic-update-slice_fusion.12), channel_id=1, source_target_pairs={{0,4},{1,5},{2,6},{3,7},{4,0},{5,1},{6,2},{7,3},{8,12},{9,13},{10,... | collective-permute-start | bytes 393224 | tf_op jit(solution)/shard_map/ppermute | solution.py:57
  282.0 6.5 %collective-permute-start.40 = (bf16[512,256]{1,0:T(8,128)(2,1)S(1)}, bf16[512,256]{1,0:T(8,128)(2,1)S(1)}, u32[]{:S(2)}, u32[]{:S(2)}) collective-permute-start(bf16[512,256]{1,0:T(8,128)(2,1)S(1)} %constant_dynamic-update-slice_fusion.10), channel_id=1, source_target_pairs={{0,2},{1,3},{2,0},{3,1},{4,6},{5,7},{6,4},{7,5},{8,10},{9,11},{10,... | collective-permute-start | bytes 786440 | tf_op jit(solution)/shard_map/ppermute | solution.py:57
  288.5 2.0 collective-permute-start.41
  291.8 8.4 %collective-permute-start.49 = (bf16[512,256]{1,0:T(8,128)(2,1)S(1)}, bf16[512,256]{1,0:T(8,128)(2,1)S(1)}, u32[]{:S(2)}, u32[]{:S(2)}) collective-permute-start(bf16[512,256]{1,0:T(8,128)(2,1)S(1)} %dynamic-slice_convert_fusion.2), channel_id=1, source_target_pairs={{0,32},{16,48},{32,0},{48,16},{64,96},{80,112},{96,64},{112,80},{1... | collective-permute-start | bytes 786440 | tf_op jit(solution)/shard_map/ppermute | solution.py:49
  300.4 6.6 %collective-permute-start.50 = (bf16[256,256]{1,0:T(8,128)(2,1)S(1)}, bf16[256,256]{1,0:T(8,128)(2,1)S(1)}, u32[]{:S(2)}, u32[]{:S(2)}) collective-permute-start(bf16[256,256]{1,0:T(8,128)(2,1)S(1)} %dynamic-slice_convert_fusion.7), channel_id=1, source_target_pairs={{0,16},{16,0},{32,48},{48,32},{64,80},{80,64},{96,112},{112,96},{1... | collective-permute-start | bytes 393224 | tf_op jit(solution)/shard_map/ppermute | solution.py:49
  307.0 5.8 %collective-permute-start.51 = (bf16[128,256]{1,0:T(8,128)(2,1)S(1)}, bf16[128,256]{1,0:T(8,128)(2,1)S(1)}, u32[]{:S(2)}, u32[]{:S(2)}) collective-permute-start(bf16[128,256]{1,0:T(8,128)(2,1)S(1)} %dynamic-slice_convert_fusion.12), channel_id=1, source_target_pairs={{0,64},{16,80},{32,96},{48,112},{64,0},{80,16},{96,32},{112,48},{1... | collective-permute-start | bytes 196616 | tf_op jit(solution)/shard_map/ppermute | solution.py:49
  312.9 6.6 %collective-permute-start.52 = (f32[128,256]{1,0:T(8,128)S(1)}, f32[128,256]{1,0:T(8,128)S(1)}, u32[]{:S(2)}, u32[]{:S(2)}) collective-permute-start(f32[128,256]{1,0:T(8,128)S(1)} %get-tuple-element.3), channel_id=1, source_target_pairs={{0,64},{16,80},{32,96},{48,112},{64,0},{80,16},{96,32},{112,48},{1... | collective-permute-start | bytes 393224 | tf_op jit(solution)/shard_map/ppermute | solution.py:57
  319.5 8.0 %collective-permute-start.53 = (f32[256,256]{1,0:T(8,128)S(1)}, f32[256,256]{1,0:T(8,128)S(1)}, u32[]{:S(2)}, u32[]{:S(2)}) collective-permute-start(f32[256,256]{1,0:T(8,128)S(1)} %constant_dynamic-update-slice_fusion.4), channel_id=1, source_target_pairs={{0,16},{16,0},{32,48},{48,32},{64,80},{80,64},{96,112},{112,96},{1... | collective-permute-start | bytes 786440 | tf_op jit(solution)/shard_map/ppermute | solution.py:57
  321.6 1.2 collective-permute-start.45
  322.9 7.0 %collective-permute-start.46 = (f32[256]{0:T(256)S(1)}, f32[256]{0:T(256)S(1)}, u32[]{:S(2)}, u32[]{:S(2)}) collective-permute-start(f32[256]{0:T(256)S(1)} %add.353), channel_id=1, source_target_pairs={{0,2},{1,3},{2,0},{3,1},{4,6},{5,7},{6,4},{7,5},{8,10},{9,11},{10,... | collective-permute-start | bytes 3080 | tf_op jit(solution)/shard_map/ppermute | solution.py:49
  327.4 21.1 %collective-permute-start.54 = (f32[512,256]{1,0:T(8,128)S(1)}, f32[512,256]{1,0:T(8,128)S(1)}, u32[]{:S(2)}, u32[]{:S(2)}) collective-permute-start(f32[512,256]{1,0:T(8,128)S(1)} %constant_dynamic-update-slice_fusion.2), channel_id=1, source_target_pairs={{0,32},{16,48},{32,0},{48,16},{64,96},{80,112},{96,64},{112,80},{1... | collective-permute-start | bytes 1572872 | tf_op jit(solution)/shard_map/ppermute | solution.py:57
  328.8 9.5 %collective-permute-start.42 = (f32[256]{0:T(256)S(1)}, f32[256]{0:T(256)S(1)}, u32[]{:S(2)}, u32[]{:S(2)}) collective-permute-start(f32[256]{0:T(256)S(1)} %multiply_reduce_fusion), channel_id=1, source_target_pairs={{0,32},{16,48},{32,0},{48,16},{64,96},{80,112},{96,64},{112,80},{1... | collective-permute-start | bytes 3080 | tf_op jit(solution)/shard_map/ppermute | solution.py:49
  329.9 11.4 %collective-permute-start.47 = (f32[256]{0:T(256)S(1)}, f32[256]{0:T(256)S(1)}, u32[]{:S(2)}, u32[]{:S(2)}) collective-permute-start(f32[256]{0:T(256)S(1)} %add.354), channel_id=1, source_target_pairs={{0,4},{1,5},{2,6},{3,7},{4,0},{5,1},{6,2},{7,3},{8,12},{9,13},{10,... | collective-permute-start | bytes 3080 | tf_op jit(solution)/shard_map/ppermute | solution.py:49
  338.3 5.1 %collective-permute-start.43 = (f32[256]{0:T(256)S(1)}, f32[256]{0:T(256)S(1)}, u32[]{:S(2)}, u32[]{:S(2)}) collective-permute-start(f32[256]{0:T(256)S(1)} %add.350), channel_id=1, source_target_pairs={{0,16},{16,0},{32,48},{48,32},{64,80},{80,64},{96,112},{112,96},{1... | collective-permute-start | bytes 3080 | tf_op jit(solution)/shard_map/ppermute | solution.py:49
  341.3 5.1 %collective-permute-start.48 = (f32[256]{0:T(256)S(1)}, f32[256]{0:T(256)S(1)}, u32[]{:S(2)}, u32[]{:S(2)}) collective-permute-start(f32[256]{0:T(256)S(1)} %add.355), channel_id=1, source_target_pairs={{0,8},{1,9},{2,10},{3,11},{4,12},{5,13},{6,14},{7,15},{8,0},{9,1},... | collective-permute-start | bytes 3080 | tf_op jit(solution)/shard_map/ppermute | solution.py:49
  343.3 5.1 %collective-permute-start.44 = (f32[256]{0:T(256)S(1)}, f32[256]{0:T(256)S(1)}, u32[]{:S(2)}, u32[]{:S(2)}) collective-permute-start(f32[256]{0:T(256)S(1)} %add.351), channel_id=1, source_target_pairs={{0,64},{16,80},{32,96},{48,112},{64,0},{80,16},{96,32},{112,48},{1... | collective-permute-start | bytes 3080 | tf_op jit(solution)/shard_map/ppermute | solution.py:49
Sparse Core Ops, SparseCore 0:
  9.7 39.8 all-gather.1

commit v3 on v2

--- a/solution.py
+++ b/solution.py
@@ -76,7 +76,9 @@
     column_mean = butterfly_sum(jnp.sum(raw, axis=0), "sample", sample_bits) / n_rows
     kernel = (raw - column_mean[None, :]).astype(jnp.bfloat16)
     rhs_part = jnp.dot(kernel.T, targets, preferred_element_type=jnp.float32)
-    rhs_total, _ = halving_sum(rhs_part, jnp.zeros((1,), jnp.float32), "sample", sample_bits, jnp.float32)
+    rhs_total, _ = halving_sum(
+        rhs_part, jnp.zeros((1,), jnp.float32), "sample", sample_bits, jnp.float32, jnp.float32
+    )
     rhs = rhs_total / math.sqrt(n_rows)
     weights = jnp.zeros_like(rhs)
     residual = rhs
@@ -98,7 +100,7 @@
         row_square = jnp.sum(jnp.square(row_half.astype(jnp.float32)), axis=0)
         column_part = jnp.dot(kernel.T, row_half, preferred_element_type=jnp.float32)
         column_total, row_square_total = halving_sum(
-            column_part, row_square, "sample", sample_bits, jnp.float32
+            column_part, row_square, "sample", sample_bits, jnp.float32, jnp.float32
         )
         image = column_total / n_rows + ridge * direction
         curvature = row_square_total / n_rows + ridge * direction_square

time: 358 us -> 381 us (1.064)
  waiting for transfers between devices: 194 us -> 219 us
    ppermute x31, waiting for transfers between devices: 98.7 us -> 123 us  [halving_sum(): got, got_extra = lax.ppermute((send.astype(wire_dtype), extra), axis, perm)]
where the time goes in v3:
time: 381 us
  waiting for transfers between devices  219 us (57%)
  starting transfers between devices  95.6 us (25%)
  local copies, waits for them, and re-layouts  20 us (5%)
  matrix products  19.7 us (5%)
  between operations  14.8 us (4%)
  other arithmetic  11.8 us (3%)
    ppermute x31, waiting for transfers between devices, halving_sum(): got, got_extra = lax.ppermute((send.astype(wire_dtype), extra), axis, perm)  123 us
    ppermute x17, waiting for transfers between devices, halving_sum(): got = lax.ppermute(x, axis, perm)  53.5 us
    ppermute x31, starting transfers between devices, halving_sum(): got, got_extra = lax.ppermute((send.astype(wire_dtype), extra), axis, perm)  50.8 us
    ppermute x17, starting transfers between devices, halving_sum(): got = lax.ppermute(x, axis, perm)  32.4 us
    all_gather x1, waiting for transfers between devices, on_device(): gathered = lax.all_gather(summaries, 'landmark', axis=1, tiled=True)  26.2 us
    ppermute x7, waiting for transfers between devices, butterfly_sum(): x = x + lax.ppermute(x, axis, perm)  15 us
    ppermute x7, starting transfers between devices, butterfly_sum(): x = x + lax.ppermute(x, axis, perm)  12.3 us
    dot_general x1, matrix products, raw_block(): jnp.dot(summary_rows, anchors.T, preferred_element_type=jnp.float32)  10.9 us
  transfers between devices with their start and end apart: 56, of which 49 were waited for; matrix products, arithmetic and copies ran while one was open for 5% of the time, Pallas kernels for 0%

profile of v3, /device:TPU:0, one launch (start us, length us, event | category | flops | bytes accessed | tf_op | source)
XLA Modules:
  0.0 380.7 jit_solution(17816834823472426476)
XLA Ops:
  8.6 5.7 %gather_fusion.1 = s32[1024]{0:T(1024)S(1)} fusion(s32[2048]{0:T(1024)} %param.10, s32[1024]{0:T(1024)S(1)} %fusion.9), kind=kCustom, calls=%fused_computation.1 | custom fusion | bytes 12288 | tf_op jit(solution)/shard_map/jit(_take)/gather | solution.py:72
  14.4 8.8 %gather_fusion = bf16[1024,1024]{1,0:T(8,128)(2,1)} fusion(bf16[2048,1024]{1,0:T(8,128)(2,1)} %param.9, s32[1024]{0:T(1024)S(1)} %fusion.9), kind=kCustom, calls=%fused_computation | custom fusion | bytes 4198400 | tf_op jit(solution)/shard_map/jit(_take)/gather | solution.py:71
  23.4 26.2 %all-gather.2.cloned.1.call-done = bf16[2048,1024]{0,1:T(8,128)(2,1)} async-done(((bf16[2048,64]{0,1:T(8,128)(2,1)}), bf16[2048,1024]{0,1:T(8,128)(2,1)}) %all-gather.2.cloned.1.call-update) | async-done | bytes 4194320 | tf_op jit(solution)/shard_map/all_gather | solution.py:69
  49.6 10.9 %fusion = (f32[1024]{0:T(1024)S(1)}, f32[1024,2048]{1,0:T(8,128)}) fusion(f32[1024]{0:T(1024)S(1)} %broadcast_divide_fusion.1, f32[2048]{0:T(1024)S(1)} %broadcast_divide_fusion, bf16[2048,1024]{0,1:T(8,128)(2,1)} %all-gather.2.cloned.1.call-done, bf16[1024,1024]{1,0:T(8,128)(2,1)} %gather_fusion, pred[1024]{0:T(1024)(128)(4,1)S(1)} %get-tuple-element.17), kind=kOutput, calls=%fused_computation.4 | convolution fusion | flops 4302306304 | bytes 14697472 | tf_op jit(solution)/shard_map/dot_general | solution.py:22
  62.0 2.1 collective-permute-done
  64.1 2.8 collective-permute-start.1
  66.9 2.3 collective-permute-done.1
  69.2 2.9 collective-permute-start.2
  72.1 2.2 collective-permute-done.2
  74.3 4.3 %subtract_convert_fusion = bf16[1024,2048]{1,0:T(8,128)(2,1)S(1)} fusion(f32[1024,2048]{1,0:T(8,128)} %get-tuple-element.21, f32[1024]{0:T(1024)S(1)} %add_multiply_fusion, f32[1024]{0:T(1024)S(1)} %broadcast_divide_fusion.1, f32[2048]{0:T(1024)S(1)} %broadcast_divide_fusion), kind=kLoop, calls=%fused_computation.2 | loop fusion | flops 8388608 | bytes 12599296 | tf_op jit(solution)/shard_map/convert
  82.1 9.1 %collective-permute-done.3 = f32[512,256]{1,0:T(8,128)S(1)} collective-permute-done((f32[512,256]{1,0:T(8,128)S(1)}, f32[512,256]{1,0:T(8,128)S(1)}, u32[]{:S(2)}, u32[]{:S(2)}) %collective-permute-start.3) | collective-permute-done | bytes 524320 | tf_op jit(solution)/shard_map/ppermute | solution.py:49
  91.3 2.8 collective-permute-start.4
  94.2 5.1 %collective-permute-done.4 = f32[256,256]{1,0:T(8,128)S(1)} collective-permute-done((f32[256,256]{1,0:T(8,128)S(1)}, f32[256,256]{1,0:T(8,128)S(1)}, u32[]{:S(2)}, u32[]{:S(2)}) %collective-permute-start.4) | collective-permute-done | bytes 262176 | tf_op jit(solution)/shard_map/ppermute | solution.py:49
  99.4 3.0 collective-permute-start.5
  102.3 4.2 %collective-permute-done.5 = f32[128,256]{1,0:T(8,128)S(1)} collective-permute-done((f32[128,256]{1,0:T(8,128)S(1)}, f32[128,256]{1,0:T(8,128)S(1)}, u32[]{:S(2)}, u32[]{:S(2)}) %collective-permute-start.5) | collective-permute-done | bytes 131104 | tf_op jit(solution)/shard_map/ppermute | solution.py:49
  106.6 3.0 collective-permute-start.6
  109.6 3.6 collective-permute-done.6
  113.2 2.8 collective-permute-start.7
  116.1 5.0 %collective-permute-done.7 = f32[256,256]{1,0:T(8,128)S(1)} collective-permute-done((f32[256,256]{1,0:T(8,128)S(1)}, f32[256,256]{1,0:T(8,128)S(1)}, u32[]{:S(2)}, u32[]{:S(2)}) %collective-permute-start.7) | collective-permute-done | bytes 262176 | tf_op jit(solution)/shard_map/ppermute | solution.py:57
  123.1 7.6 %collective-permute-done.8 = f32[512,256]{1,0:T(8,128)S(1)} collective-permute-done((f32[512,256]{1,0:T(8,128)S(1)}, f32[512,256]{1,0:T(8,128)S(1)}, u32[]{:S(2)}, u32[]{:S(2)}) %collective-permute-start.8) | collective-permute-done | bytes 524320 | tf_op jit(solution)/shard_map/ppermute | solution.py:57
  130.7 3.5 fusion.5
  141.2 7.3 %collective-permute-done.14 = bf16[512,256]{1,0:T(8,128)(2,1)S(1)} collective-permute-done((bf16[512,256]{1,0:T(8,128)(2,1)}, bf16[512,256]{1,0:T(8,128)(2,1)S(1)}, u32[]{:S(2)}, u32[]{:S(2)}) %collective-permute-start.14) | collective-permute-done | bytes 262176 | tf_op jit(solution)/shard_map/ppermute | solution.py:49
  150.7 3.8 collective-permute-done.15
  155.5 2.1 collective-permute-start.16
  157.5 3.8 collective-permute-done.16
  161.4 2.1 collective-permute-start.17
  163.4 4.0 %collective-permute-done.17 = bf16[128,256]{1,0:T(8,128)(2,1)S(1)} collective-permute-done((bf16[128,256]{1,0:T(8,128)(2,1)S(1)}, bf16[128,256]{1,0:T(8,128)(2,1)S(1)}, u32[]{:S(2)}, u32[]{:S(2)}) %collective-permute-start.17) | collective-permute-done | bytes 65568 | tf_op jit(solution)/shard_map/ppermute | solution.py:57
  169.3 3.2 collective-permute-done.18
  174.3 4.6 %collective-permute-done.19 = bf16[512,256]{1,0:T(8,128)(2,1)S(1)} collective-permute-done((bf16[512,256]{1,0:T(8,128)(2,1)S(1)}, bf16[512,256]{1,0:T(8,128)(2,1)S(1)}, u32[]{:S(2)}, u32[]{:S(2)}) %collective-permute-start.19) | collective-permute-done | bytes 262176 | tf_op jit(solution)/shard_map/ppermute | solution.py:57
  184.1 12.2 %collective-permute-done.24 = f32[512,256]{1,0:T(8,128)S(1)} collective-permute-done((f32[512,256]{1,0:T(8,128)S(1)}, f32[512,256]{1,0:T(8,128)S(1)}, u32[]{:S(2)}, u32[]{:S(2)}) %collective-permute-start.24) | collective-permute-done | bytes 524320 | tf_op jit(solution)/shard_map/ppermute | solution.py:49
  196.5 3.2 collective-permute-start.25
  199.7 5.9 %collective-permute-done.25 = f32[256,256]{1,0:T(8,128)S(1)} collective-permute-done((f32[256,256]{1,0:T(8,128)S(1)}, f32[256,256]{1,0:T(8,128)S(1)}, u32[]{:S(2)}, u32[]{:S(2)}) %collective-permute-start.25) | collective-permute-done | bytes 262176 | tf_op jit(solution)/shard_map/ppermute | solution.py:49
  205.6 2.9 collective-permute-start.26
  208.6 3.6 collective-permute-done.26
  212.2 2.9 collective-permute-start.27
  215.4 3.3 collective-permute-done.27
  218.8 3.2 collective-permute-start.28
  222.7 4.3 %collective-permute-done.10 = f32[512]{0:T(512)S(1)} collective-permute-done((f32[512]{0:T(512)S(1)}, f32[512]{0:T(512)S(1)}, u32[]{:S(2)}, u32[]{:S(2)}) %collective-permute-start.10) | collective-permute-done | bytes 2080 | tf_op jit(solution)/shard_map/ppermute | solution.py:49
  230.6 2.1 collective-permute-start.12
  232.7 5.0 %collective-permute-done.21 = f32[256]{0:T(256)S(1)} collective-permute-done((f32[256]{0:T(256)S(1)}, f32[256]{0:T(256)S(1)}, u32[]{:S(2)}, u32[]{:S(2)}) %collective-permute-start.21) | collective-permute-done | bytes 1056 | tf_op jit(solution)/shard_map/ppermute | solution.py:49
  239.8 3.1 collective-permute-done.22
  242.8 2.5 collective-permute-start.23
  245.3 2.6 collective-permute-done.23
  254.5 2.4 collective-permute-done.32
  258.9 3.0 collective-permute-done.33
  267.6 6.6 %collective-permute-done.35 = bf16[512,256]{1,0:T(8,128)(2,1)S(1)} collective-permute-done((bf16[512,256]{1,0:T(8,128)(2,1)S(1)}, bf16[512,256]{1,0:T(8,128)(2,1)S(1)}, u32[]{:S(2)}, u32[]{:S(2)}) %collective-permute-start.35) | collective-permute-done | bytes 262176 | tf_op jit(solution)/shard_map/ppermute | solution.py:49
  275.5 3.9 %collective-permute-done.36 = bf16[256,256]{1,0:T(8,128)(2,1)S(1)} collective-permute-done((bf16[256,256]{1,0:T(8,128)(2,1)S(1)}, bf16[256,256]{1,0:T(8,128)(2,1)S(1)}, u32[]{:S(2)}, u32[]{:S(2)}) %collective-permute-start.36) | collective-permute-done | bytes 131104 | tf_op jit(solution)/shard_map/ppermute | solution.py:49
  279.4 2.3 collective-permute-start.37
  281.7 3.6 collective-permute-done.37
  285.3 2.3 collective-permute-start.38
  287.6 3.9 %collective-permute-done.38 = bf16[128,256]{1,0:T(8,128)(2,1)S(1)} collective-permute-done((bf16[128,256]{1,0:T(8,128)(2,1)S(1)}, bf16[128,256]{1,0:T(8,128)(2,1)S(1)}, u32[]{:S(2)}, u32[]{:S(2)}) %collective-permute-start.38) | collective-permute-done | bytes 65568 | tf_op jit(solution)/shard_map/ppermute | solution.py:57
  293.1 3.4 collective-permute-done.39
  296.5 2.1 collective-permute-start.40
  298.7 4.3 %collective-permute-done.40 = bf16[512,256]{1,0:T(8,128)(2,1)S(1)} collective-permute-done((bf16[512,256]{1,0:T(8,128)(2,1)S(1)}, bf16[512,256]{1,0:T(8,128)(2,1)S(1)}, u32[]{:S(2)}, u32[]{:S(2)}) %collective-permute-start.40) | collective-permute-done | bytes 262176 | tf_op jit(solution)/shard_map/ppermute | solution.py:57
  307.4 13.0 %collective-permute-done.49 = f32[512,256]{1,0:T(8,128)S(1)} collective-permute-done((f32[512,256]{1,0:T(8,128)S(1)}, f32[512,256]{1,0:T(8,128)S(1)}, u32[]{:S(2)}, u32[]{:S(2)}) %collective-permute-start.49) | collective-permute-done | bytes 524320 | tf_op jit(solution)/shard_map/ppermute | solution.py:49
  322.3 7.3 %collective-permute-done.50 = f32[256,256]{1,0:T(8,128)S(1)} collective-permute-done((f32[256,256]{1,0:T(8,128)S(1)}, f32[256,256]{1,0:T(8,128)S(1)}, u32[]{:S(2)}, u32[]{:S(2)}) %collective-permute-start.50) | collective-permute-done | bytes 262176 | tf_op jit(solution)/shard_map/ppermute | solution.py:49
  329.7 2.6 collective-permute-start.51
  332.2 4.0 %collective-permute-done.51 = f32[128,256]{1,0:T(8,128)S(1)} collective-permute-done((f32[128,256]{1,0:T(8,128)S(1)}, f32[128,256]{1,0:T(8,128)S(1)}, u32[]{:S(2)}, u32[]{:S(2)}) %collective-permute-start.51) | collective-permute-done | bytes 131104 | tf_op jit(solution)/shard_map/ppermute | solution.py:49
  336.3 2.6 collective-permute-start.52
  338.9 4.0 %collective-permute-done.52 = f32[128,256]{1,0:T(8,128)S(1)} collective-permute-done((f32[128,256]{1,0:T(8,128)S(1)}, f32[128,256]{1,0:T(8,128)S(1)}, u32[]{:S(2)}, u32[]{:S(2)}) %collective-permute-start.52) | collective-permute-done | bytes 131104 | tf_op jit(solution)/shard_map/ppermute | solution.py:57
  347.7 3.1 collective-permute-done.53
  354.8 6.9 %collective-permute-done.42 = f32[256]{0:T(256)S(1)} collective-permute-done((f32[256]{0:T(256)S(1)}, f32[256]{0:T(256)S(1)}, u32[]{:S(2)}, u32[]{:S(2)}) %collective-permute-start.42) | collective-permute-done | bytes 1056 | tf_op jit(solution)/shard_map/ppermute | solution.py:49
  361.7 3.0 collective-permute-start.43
  366.7 2.3 collective-permute-start.44
  (187 shorter events, 73.7 us)
Async XLA Ops:
  7.2 71.5 %copy-start = (bf16[2048,256]{1,0:T(8,128)(2,1)S(1)}, bf16[2048,256]{1,0:T(8,128)(2,1)}, u32[]{:S(2)}) copy-start(bf16[2048,256]{1,0:T(8,128)(2,1)} %param.13) | copy-start | bytes 3145732
  7.2 42.4 %all-gather.2.cloned.1.call-start = ((), (), s32[]{:S(2)}) async-start(), calls=%async_computation | async-start | bytes 4456448 | tf_op jit(solution)/shard_map/all_gather | solution.py:69
  14.3 8.8 %copy-start.5 = (s32[1024]{0:T(1024)S(1)}, s32[1024]{0:T(1024)}, u32[]{:S(2)}) copy-start(s32[1024]{0:T(1024)} %param.11) | copy-start | bytes 12292
  14.4 8.8 %copy-start.7 = (f32[4]{0:T(128)S(1)}, f32[4]{0:T(128)}, u32[]{:S(2)}) copy-start(f32[4]{0:T(128)} %param.12) | copy-start | bytes 52
  14.4 8.9 %copy-start.6 = (s32[2048]{0:T(1024)S(1)}, s32[2048]{0:T(1024)}, u32[]{:S(2)}) copy-start(s32[2048]{0:T(1024)} %param.8) | copy-start | bytes 24580
  60.5 3.6 collective-permute-start
  64.1 5.1 %collective-permute-start.1 = (f32[1024]{0:T(1024)S(1)}, f32[1024]{0:T(1024)S(1)}, u32[]{:S(2)}, u32[]{:S(2)}) collective-permute-start(f32[1024]{0:T(1024)S(1)} %add.298), channel_id=1, source_target_pairs={{0,16},{16,0},{32,48},{48,32},{64,80},{80,64},{96,112},{112,96},{1... | collective-permute-start | bytes 12296 | tf_op jit(solution)/shard_map/ppermute | solution.py:36
  69.2 5.1 %collective-permute-start.2 = (f32[1024]{0:T(1024)S(1)}, f32[1024]{0:T(1024)S(1)}, u32[]{:S(2)}, u32[]{:S(2)}) collective-permute-start(f32[1024]{0:T(1024)S(1)} %add.299), channel_id=1, source_target_pairs={{0,64},{16,80},{32,96},{48,112},{64,0},{80,16},{96,32},{112,48},{1... | collective-permute-start | bytes 12296 | tf_op jit(solution)/shard_map/ppermute | solution.py:36
  78.7 2.0 copy-start.1
  80.6 10.6 %collective-permute-start.3 = (f32[512,256]{1,0:T(8,128)S(1)}, f32[512,256]{1,0:T(8,128)S(1)}, u32[]{:S(2)}, u32[]{:S(2)}) collective-permute-start(f32[512,256]{1,0:T(8,128)S(1)} %constant_dynamic-slice_fusion.8), channel_id=1, source_target_pairs={{0,32},{16,48},{32,0},{48,16},{64,96},{80,112},{96,64},{112,80},{1... | collective-permute-start | bytes 1572872 | tf_op jit(solution)/shard_map/ppermute | solution.py:49
  91.3 8.0 %collective-permute-start.4 = (f32[256,256]{1,0:T(8,128)S(1)}, f32[256,256]{1,0:T(8,128)S(1)}, u32[]{:S(2)}, u32[]{:S(2)}) collective-permute-start(f32[256,256]{1,0:T(8,128)S(1)} %constant_dynamic-slice_fusion.7), channel_id=1, source_target_pairs={{0,16},{16,0},{32,48},{48,32},{64,80},{80,64},{96,112},{112,96},{1... | collective-permute-start | bytes 786440 | tf_op jit(solution)/shard_map/ppermute | solution.py:49
  99.4 7.2 %collective-permute-start.5 = (f32[128,256]{1,0:T(8,128)S(1)}, f32[128,256]{1,0:T(8,128)S(1)}, u32[]{:S(2)}, u32[]{:S(2)}) collective-permute-start(f32[128,256]{1,0:T(8,128)S(1)} %constant_dynamic-slice_fusion.6), channel_id=1, source_target_pairs={{0,64},{16,80},{32,96},{48,112},{64,0},{80,16},{96,32},{112,48},{1... | collective-permute-start | bytes 393224 | tf_op jit(solution)/shard_map/ppermute | solution.py:49
  106.6 6.6 %collective-permute-start.6 = (f32[128,256]{1,0:T(8,128)S(1)}, f32[128,256]{1,0:T(8,128)S(1)}, u32[]{:S(2)}, u32[]{:S(2)}) collective-permute-start(f32[128,256]{1,0:T(8,128)S(1)} %get-tuple-element.15), channel_id=1, source_target_pairs={{0,64},{16,80},{32,96},{48,112},{64,0},{80,16},{96,32},{112,48},{1... | collective-permute-start | bytes 393224 | tf_op jit(solution)/shard_map/ppermute | solution.py:57
  113.2 8.0 %collective-permute-start.7 = (f32[256,256]{1,0:T(8,128)S(1)}, f32[256,256]{1,0:T(8,128)S(1)}, u32[]{:S(2)}, u32[]{:S(2)}) collective-permute-start(f32[256,256]{1,0:T(8,128)S(1)} %constant_dynamic-update-slice_fusion.32), channel_id=1, source_target_pairs={{0,16},{16,0},{32,48},{48,32},{64,80},{80,64},{96,112},{112,96},{1... | collective-permute-start | bytes 786440 | tf_op jit(solution)/shard_map/ppermute | solution.py:57
  121.2 9.4 %collective-permute-start.8 = (f32[512,256]{1,0:T(8,128)S(1)}, f32[512,256]{1,0:T(8,128)S(1)}, u32[]{:S(2)}, u32[]{:S(2)}) collective-permute-start(f32[512,256]{1,0:T(8,128)S(1)} %constant_dynamic-update-slice_fusion.30), channel_id=1, source_target_pairs={{0,32},{16,48},{32,0},{48,16},{64,96},{80,112},{96,64},{112,80},{1... | collective-permute-start | bytes 1572872 | tf_op jit(solution)/shard_map/ppermute | solution.py:57
  134.2 1.4 copy-start.4
  135.6 2.1 collective-permute-start.13
  140.0 8.6 %collective-permute-start.14 = (bf16[512,256]{1,0:T(8,128)(2,1)}, bf16[512,256]{1,0:T(8,128)(2,1)S(1)}, u32[]{:S(2)}, u32[]{:S(2)}) collective-permute-start(bf16[512,256]{1,0:T(8,128)(2,1)} %dynamic-slice_convert_fusion.3), channel_id=1, source_target_pairs={{0,2},{1,3},{2,0},{3,1},{4,6},{5,7},{6,4},{7,5},{8,10},{9,11},{10,... | collective-permute-start | bytes 786440 | tf_op jit(solution)/shard_map/ppermute | solution.py:49
  148.6 0.8 copy-start.3
  149.4 5.0 %collective-permute-start.15 = (bf16[256,256]{1,0:T(8,128)(2,1)S(1)}, bf16[256,256]{1,0:T(8,128)(2,1)S(1)}, u32[]{:S(2)}, u32[]{:S(2)}) collective-permute-start(bf16[256,256]{1,0:T(8,128)(2,1)S(1)} %dynamic-slice_convert_fusion.5), channel_id=1, source_target_pairs={{0,4},{1,5},{2,6},{3,7},{4,0},{5,1},{6,2},{7,3},{8,12},{9,13},{10,... | collective-permute-start | bytes 393224 | tf_op jit(solution)/shard_map/ppermute | solution.py:49
  155.5 5.8 %collective-permute-start.16 = (bf16[128,256]{1,0:T(8,128)(2,1)S(1)}, bf16[128,256]{1,0:T(8,128)(2,1)S(1)}, u32[]{:S(2)}, u32[]{:S(2)}) collective-permute-start(bf16[128,256]{1,0:T(8,128)(2,1)S(1)} %dynamic-slice_convert_fusion.7), channel_id=1, source_target_pairs={{0,8},{1,9},{2,10},{3,11},{4,12},{5,13},{6,14},{7,15},{8,0},{9,1},... | collective-permute-start | bytes 196616 | tf_op jit(solution)/shard_map/ppermute | solution.py:49
  157.5 23.5 %copy-start.2 = (bf16[1024,2048]{1,0:T(8,128)(2,1)S(1)}, bf16[1024,2048]{1,0:T(8,128)(2,1)}, u32[]{:S(2)}) copy-start(bf16[1024,2048]{1,0:T(8,128)(2,1)} %copy-done.1) | copy-start | bytes 12582916
  161.4 6.1 %collective-permute-start.17 = (bf16[128,256]{1,0:T(8,128)(2,1)S(1)}, bf16[128,256]{1,0:T(8,128)(2,1)S(1)}, u32[]{:S(2)}, u32[]{:S(2)}) collective-permute-start(bf16[128,256]{1,0:T(8,128)(2,1)S(1)} %get-tuple-element.13), channel_id=1, source_target_pairs={{0,8},{1,9},{2,10},{3,11},{4,12},{5,13},{6,14},{7,15},{8,0},{9,1},... | collective-permute-start | bytes 196616 | tf_op jit(solution)/shard_map/ppermute | solution.py:57
  167.4 5.0 %collective-permute-start.18 = (bf16[256,256]{1,0:T(8,128)(2,1)S(1)}, bf16[256,256]{1,0:T(8,128)(2,1)S(1)}, u32[]{:S(2)}, u32[]{:S(2)}) collective-permute-start(bf16[256,256]{1,0:T(8,128)(2,1)S(1)} %constant_dynamic-update-slice_fusion.26), channel_id=1, source_target_pairs={{0,4},{1,5},{2,6},{3,7},{4,0},{5,1},{6,2},{7,3},{8,12},{9,13},{10,... | collective-permute-start | bytes 393224 | tf_op jit(solution)/shard_map/ppermute | solution.py:57
  172.5 6.5 %collective-permute-start.19 = (bf16[512,256]{1,0:T(8,128)(2,1)S(1)}, bf16[512,256]{1,0:T(8,128)(2,1)S(1)}, u32[]{:S(2)}, u32[]{:S(2)}) collective-permute-start(bf16[512,256]{1,0:T(8,128)(2,1)S(1)} %constant_dynamic-update-slice_fusion.24), channel_id=1, source_target_pairs={{0,2},{1,3},{2,0},{3,1},{4,6},{5,7},{6,4},{7,5},{8,10},{9,11},{10,... | collective-permute-start | bytes 786440 | tf_op jit(solution)/shard_map/ppermute | solution.py:57
  179.0 2.0 collective-permute-start.20
  182.3 14.0 %collective-permute-start.24 = (f32[512,256]{1,0:T(8,128)S(1)}, f32[512,256]{1,0:T(8,128)S(1)}, u32[]{:S(2)}, u32[]{:S(2)}) collective-permute-start(f32[512,256]{1,0:T(8,128)S(1)} %constant_dynamic-slice_fusion.5), channel_id=1, source_target_pairs={{0,32},{16,48},{32,0},{48,16},{64,96},{80,112},{96,64},{112,80},{1... | collective-permute-start | bytes 1572872 | tf_op jit(solution)/shard_map/ppermute | solution.py:49
  196.5 9.1 %collective-permute-start.25 = (f32[256,256]{1,0:T(8,128)S(1)}, f32[256,256]{1,0:T(8,128)S(1)}, u32[]{:S(2)}, u32[]{:S(2)}) collective-permute-start(f32[256,256]{1,0:T(8,128)S(1)} %constant_dynamic-slice_fusion.4), channel_id=1, source_target_pairs={{0,16},{16,0},{32,48},{48,32},{64,80},{80,64},{96,112},{112,96},{1... | collective-permute-start | bytes 786440 | tf_op jit(solution)/shard_map/ppermute | solution.py:49
  205.6 6.6 %collective-permute-start.26 = (f32[128,256]{1,0:T(8,128)S(1)}, f32[128,256]{1,0:T(8,128)S(1)}, u32[]{:S(2)}, u32[]{:S(2)}) collective-permute-start(f32[128,256]{1,0:T(8,128)S(1)} %constant_dynamic-slice_fusion.3), channel_id=1, source_target_pairs={{0,64},{16,80},{32,96},{48,112},{64,0},{80,16},{96,32},{112,48},{1... | collective-permute-start | bytes 393224 | tf_op jit(solution)/shard_map/ppermute | solution.py:49
  212.2 6.6 %collective-permute-start.27 = (f32[128,256]{1,0:T(8,128)S(1)}, f32[128,256]{1,0:T(8,128)S(1)}, u32[]{:S(2)}, u32[]{:S(2)}) collective-permute-start(f32[128,256]{1,0:T(8,128)S(1)} %get-tuple-element.11), channel_id=1, source_target_pairs={{0,64},{16,80},{32,96},{48,112},{64,0},{80,16},{96,32},{112,48},{1... | collective-permute-start | bytes 393224 | tf_op jit(solution)/shard_map/ppermute | solution.py:57
  215.4 6.7 %collective-permute-start.9 = (f32[512]{0:T(512)S(1)}, f32[512]{0:T(512)S(1)}, u32[]{:S(2)}, u32[]{:S(2)}) collective-permute-start(f32[512]{0:T(512)S(1)} %pad_maximum_fusion), channel_id=1, source_target_pairs={{0,1},{1,0},{2,3},{3,2},{4,5},{5,4},{6,7},{7,6},{8,9},{9,8},{10,11... | collective-permute-start | bytes 6152 | tf_op jit(solution)/shard_map/ppermute | solution.py:49
  218.8 9.1 %collective-permute-start.28 = (f32[256,256]{1,0:T(8,128)S(1)}, f32[256,256]{1,0:T(8,128)S(1)}, u32[]{:S(2)}, u32[]{:S(2)}) collective-permute-start(f32[256,256]{1,0:T(8,128)S(1)} %constant_dynamic-update-slice_fusion.18), channel_id=1, source_target_pairs={{0,16},{16,0},{32,48},{48,32},{64,80},{80,64},{96,112},{112,96},{1... | collective-permute-start | bytes 786440 | tf_op jit(solution)/shard_map/ppermute | solution.py:57
  222.0 5.0 %collective-permute-start.10 = (f32[512]{0:T(512)S(1)}, f32[512]{0:T(512)S(1)}, u32[]{:S(2)}, u32[]{:S(2)}) collective-permute-start(f32[512]{0:T(512)S(1)} %fusion.12), channel_id=1, source_target_pairs={{0,2},{1,3},{2,0},{3,1},{4,6},{5,7},{6,4},{7,5},{8,10},{9,11},{10,... | collective-permute-start | bytes 6152 | tf_op jit(solution)/shard_map/ppermute | solution.py:49
  227.0 3.6 collective-permute-start.11
  227.9 20.1 %collective-permute-start.29 = (f32[512,256]{1,0:T(8,128)S(1)}, f32[512,256]{1,0:T(8,128)S(1)}, u32[]{:S(2)}, u32[]{:S(2)}) collective-permute-start(f32[512,256]{1,0:T(8,128)S(1)} %constant_dynamic-update-slice_fusion.16), channel_id=1, source_target_pairs={{0,32},{16,48},{32,0},{48,16},{64,96},{80,112},{96,64},{112,80},{1... | collective-permute-start | bytes 1572872 | tf_op jit(solution)/shard_map/ppermute | solution.py:57
  229.8 8.0 %collective-permute-start.21 = (f32[256]{0:T(256)S(1)}, f32[256]{0:T(256)S(1)}, u32[]{:S(2)}, u32[]{:S(2)}) collective-permute-start(f32[256]{0:T(256)S(1)} %multiply_reduce_fusion.1), channel_id=1, source_target_pairs={{0,32},{16,48},{32,0},{48,16},{64,96},{80,112},{96,64},{112,80},{1... | collective-permute-start | bytes 3080 | tf_op jit(solution)/shard_map/ppermute | solution.py:49
  230.6 14.7 %collective-permute-start.12 = (f32[512]{0:T(512)S(1)}, f32[512]{0:T(512)S(1)}, u32[]{:S(2)}, u32[]{:S(2)}) collective-permute-start(f32[512]{0:T(512)S(1)} %add.315), channel_id=1, source_target_pairs={{0,8},{1,9},{2,10},{3,11},{4,12},{5,13},{6,14},{7,15},{8,0},{9,1},... | collective-permute-start | bytes 6152 | tf_op jit(solution)/shard_map/ppermute | solution.py:49
  237.8 5.1 %collective-permute-start.22 = (f32[256]{0:T(256)S(1)}, f32[256]{0:T(256)S(1)}, u32[]{:S(2)}, u32[]{:S(2)}) collective-permute-start(f32[256]{0:T(256)S(1)} %add.333), channel_id=1, source_target_pairs={{0,16},{16,0},{32,48},{48,32},{64,80},{80,64},{96,112},{112,96},{1... | collective-permute-start | bytes 3080 | tf_op jit(solution)/shard_map/ppermute | solution.py:49
  242.8 5.1 %collective-permute-start.23 = (f32[256]{0:T(256)S(1)}, f32[256]{0:T(256)S(1)}, u32[]{:S(2)}, u32[]{:S(2)}) collective-permute-start(f32[256]{0:T(256)S(1)} %add.334), channel_id=1, source_target_pairs={{0,64},{16,80},{32,96},{48,112},{64,0},{80,16},{96,32},{112,48},{1... | collective-permute-start | bytes 3080 | tf_op jit(solution)/shard_map/ppermute | solution.py:49
  248.5 1.2 collective-permute-start.30
  249.7 3.6 collective-permute-start.31
  253.3 3.6 collective-permute-start.32
  256.9 5.1 %collective-permute-start.33 = (f32[256]{0:T(256)S(1)}, f32[256]{0:T(256)S(1)}, u32[]{:S(2)}, u32[]{:S(2)}) collective-permute-start(f32[256]{0:T(256)S(1)} %add.343), channel_id=1, source_target_pairs={{0,8},{1,9},{2,10},{3,11},{4,12},{5,13},{6,14},{7,15},{8,0},{9,1},... | collective-permute-start | bytes 3080 | tf_op jit(solution)/shard_map/ppermute | solution.py:36
  263.5 2.0 collective-permute-start.34
  265.6 8.5 %collective-permute-start.35 = (bf16[512,256]{1,0:T(8,128)(2,1)S(1)}, bf16[512,256]{1,0:T(8,128)(2,1)S(1)}, u32[]{:S(2)}, u32[]{:S(2)}) collective-permute-start(bf16[512,256]{1,0:T(8,128)(2,1)S(1)} %dynamic-slice_convert_fusion.2), channel_id=1, source_target_pairs={{0,2},{1,3},{2,0},{3,1},{4,6},{5,7},{6,4},{7,5},{8,10},{9,11},{10,... | collective-permute-start | bytes 786440 | tf_op jit(solution)/shard_map/ppermute | solution.py:49
  274.3 5.0 %collective-permute-start.36 = (bf16[256,256]{1,0:T(8,128)(2,1)S(1)}, bf16[256,256]{1,0:T(8,128)(2,1)S(1)}, u32[]{:S(2)}, u32[]{:S(2)}) collective-permute-start(bf16[256,256]{1,0:T(8,128)(2,1)S(1)} %dynamic-slice_convert_fusion.4), channel_id=1, source_target_pairs={{0,4},{1,5},{2,6},{3,7},{4,0},{5,1},{6,2},{7,3},{8,12},{9,13},{10,... | collective-permute-start | bytes 393224 | tf_op jit(solution)/shard_map/ppermute | solution.py:49
  279.4 5.8 %collective-permute-start.37 = (bf16[128,256]{1,0:T(8,128)(2,1)S(1)}, bf16[128,256]{1,0:T(8,128)(2,1)S(1)}, u32[]{:S(2)}, u32[]{:S(2)}) collective-permute-start(bf16[128,256]{1,0:T(8,128)(2,1)S(1)} %dynamic-slice_convert_fusion.6), channel_id=1, source_target_pairs={{0,8},{1,9},{2,10},{3,11},{4,12},{5,13},{6,14},{7,15},{8,0},{9,1},... | collective-permute-start | bytes 196616 | tf_op jit(solution)/shard_map/ppermute | solution.py:49
  285.3 6.2 %collective-permute-start.38 = (bf16[128,256]{1,0:T(8,128)(2,1)S(1)}, bf16[128,256]{1,0:T(8,128)(2,1)S(1)}, u32[]{:S(2)}, u32[]{:S(2)}) collective-permute-start(bf16[128,256]{1,0:T(8,128)(2,1)S(1)} %get-tuple-element.7), channel_id=1, source_target_pairs={{0,8},{1,9},{2,10},{3,11},{4,12},{5,13},{6,14},{7,15},{8,0},{9,1},... | collective-permute-start | bytes 196616 | tf_op jit(solution)/shard_map/ppermute | solution.py:57
  291.5 5.0 %collective-permute-start.39 = (bf16[256,256]{1,0:T(8,128)(2,1)S(1)}, bf16[256,256]{1,0:T(8,128)(2,1)S(1)}, u32[]{:S(2)}, u32[]{:S(2)}) collective-permute-start(bf16[256,256]{1,0:T(8,128)(2,1)S(1)} %constant_dynamic-update-slice_fusion.12), channel_id=1, source_target_pairs={{0,4},{1,5},{2,6},{3,7},{4,0},{5,1},{6,2},{7,3},{8,12},{9,13},{10,... | collective-permute-start | bytes 393224 | tf_op jit(solution)/shard_map/ppermute | solution.py:57
  296.5 6.5 %collective-permute-start.40 = (bf16[512,256]{1,0:T(8,128)(2,1)S(1)}, bf16[512,256]{1,0:T(8,128)(2,1)S(1)}, u32[]{:S(2)}, u32[]{:S(2)}) collective-permute-start(bf16[512,256]{1,0:T(8,128)(2,1)S(1)} %constant_dynamic-update-slice_fusion.10), channel_id=1, source_target_pairs={{0,2},{1,3},{2,0},{3,1},{4,6},{5,7},{6,4},{7,5},{8,10},{9,11},{10,... | collective-permute-start | bytes 786440 | tf_op jit(solution)/shard_map/ppermute | solution.py:57
  303.0 2.0 collective-permute-start.41
  306.4 14.0 %collective-permute-start.49 = (f32[512,256]{1,0:T(8,128)S(1)}, f32[512,256]{1,0:T(8,128)S(1)}, u32[]{:S(2)}, u32[]{:S(2)}) collective-permute-start(f32[512,256]{1,0:T(8,128)S(1)} %constant_dynamic-slice_fusion.2), channel_id=1, source_target_pairs={{0,32},{16,48},{32,0},{48,16},{64,96},{80,112},{96,64},{112,80},{1... | collective-permute-start | bytes 1572872 | tf_op jit(solution)/shard_map/ppermute | solution.py:49
  320.5 9.1 %collective-permute-start.50 = (f32[256,256]{1,0:T(8,128)S(1)}, f32[256,256]{1,0:T(8,128)S(1)}, u32[]{:S(2)}, u32[]{:S(2)}) collective-permute-start(f32[256,256]{1,0:T(8,128)S(1)} %constant_dynamic-slice_fusion.1), channel_id=1, source_target_pairs={{0,16},{16,0},{32,48},{48,32},{64,80},{80,64},{96,112},{112,96},{1... | collective-permute-start | bytes 786440 | tf_op jit(solution)/shard_map/ppermute | solution.py:49
  329.7 6.6 %collective-permute-start.51 = (f32[128,256]{1,0:T(8,128)S(1)}, f32[128,256]{1,0:T(8,128)S(1)}, u32[]{:S(2)}, u32[]{:S(2)}) collective-permute-start(f32[128,256]{1,0:T(8,128)S(1)} %constant_dynamic-slice_fusion), channel_id=1, source_target_pairs={{0,64},{16,80},{32,96},{48,112},{64,0},{80,16},{96,32},{112,48},{1... | collective-permute-start | bytes 393224 | tf_op jit(solution)/shard_map/ppermute | solution.py:49
  336.3 6.6 %collective-permute-start.52 = (f32[128,256]{1,0:T(8,128)S(1)}, f32[128,256]{1,0:T(8,128)S(1)}, u32[]{:S(2)}, u32[]{:S(2)}) collective-permute-start(f32[128,256]{1,0:T(8,128)S(1)} %get-tuple-element.3), channel_id=1, source_target_pairs={{0,64},{16,80},{32,96},{48,112},{64,0},{80,16},{96,32},{112,48},{1... | collective-permute-start | bytes 393224 | tf_op jit(solution)/shard_map/ppermute | solution.py:57
  342.9 8.0 %collective-permute-start.53 = (f32[256,256]{1,0:T(8,128)S(1)}, f32[256,256]{1,0:T(8,128)S(1)}, u32[]{:S(2)}, u32[]{:S(2)}) collective-permute-start(f32[256,256]{1,0:T(8,128)S(1)} %constant_dynamic-update-slice_fusion.4), channel_id=1, source_target_pairs={{0,16},{16,0},{32,48},{48,32},{64,80},{80,64},{96,112},{112,96},{1... | collective-permute-start | bytes 786440 | tf_op jit(solution)/shard_map/ppermute | solution.py:57
  345.0 1.2 collective-permute-start.45
  346.3 7.1 %collective-permute-start.46 = (f32[256]{0:T(256)S(1)}, f32[256]{0:T(256)S(1)}, u32[]{:S(2)}, u32[]{:S(2)}) collective-permute-start(f32[256]{0:T(256)S(1)} %add.353), channel_id=1, source_target_pairs={{0,2},{1,3},{2,0},{3,1},{4,6},{5,7},{6,4},{7,5},{8,10},{9,11},{10,... | collective-permute-start | bytes 3080 | tf_op jit(solution)/shard_map/ppermute | solution.py:49
  350.8 21.1 %collective-permute-start.54 = (f32[512,256]{1,0:T(8,128)S(1)}, f32[512,256]{1,0:T(8,128)S(1)}, u32[]{:S(2)}, u32[]{:S(2)}) collective-permute-start(f32[512,256]{1,0:T(8,128)S(1)} %constant_dynamic-update-slice_fusion.2), channel_id=1, source_target_pairs={{0,32},{16,48},{32,0},{48,16},{64,96},{80,112},{96,64},{112,80},{1... | collective-permute-start | bytes 1572872 | tf_op jit(solution)/shard_map/ppermute | solution.py:57
  352.2 9.5 %collective-permute-start.42 = (f32[256]{0:T(256)S(1)}, f32[256]{0:T(256)S(1)}, u32[]{:S(2)}, u32[]{:S(2)}) collective-permute-start(f32[256]{0:T(256)S(1)} %multiply_reduce_fusion), channel_id=1, source_target_pairs={{0,32},{16,48},{32,0},{48,16},{64,96},{80,112},{96,64},{112,80},{1... | collective-permute-start | bytes 3080 | tf_op jit(solution)/shard_map/ppermute | solution.py:49
  353.3 11.4 %collective-permute-start.47 = (f32[256]{0:T(256)S(1)}, f32[256]{0:T(256)S(1)}, u32[]{:S(2)}, u32[]{:S(2)}) collective-permute-start(f32[256]{0:T(256)S(1)} %add.354), channel_id=1, source_target_pairs={{0,4},{1,5},{2,6},{3,7},{4,0},{5,1},{6,2},{7,3},{8,12},{9,13},{10,... | collective-permute-start | bytes 3080 | tf_op jit(solution)/shard_map/ppermute | solution.py:49
  361.7 5.1 %collective-permute-start.43 = (f32[256]{0:T(256)S(1)}, f32[256]{0:T(256)S(1)}, u32[]{:S(2)}, u32[]{:S(2)}) collective-permute-start(f32[256]{0:T(256)S(1)} %add.350), channel_id=1, source_target_pairs={{0,16},{16,0},{32,48},{48,32},{64,80},{80,64},{96,112},{112,96},{1... | collective-permute-start | bytes 3080 | tf_op jit(solution)/shard_map/ppermute | solution.py:49
  364.7 5.1 %collective-permute-start.48 = (f32[256]{0:T(256)S(1)}, f32[256]{0:T(256)S(1)}, u32[]{:S(2)}, u32[]{:S(2)}) collective-permute-start(f32[256]{0:T(256)S(1)} %add.355), channel_id=1, source_target_pairs={{0,8},{1,9},{2,10},{3,11},{4,12},{5,13},{6,14},{7,15},{8,0},{9,1},... | collective-permute-start | bytes 3080 | tf_op jit(solution)/shard_map/ppermute | solution.py:49
  366.7 5.1 %collective-permute-start.44 = (f32[256]{0:T(256)S(1)}, f32[256]{0:T(256)S(1)}, u32[]{:S(2)}, u32[]{:S(2)}) collective-permute-start(f32[256]{0:T(256)S(1)} %add.351), channel_id=1, source_target_pairs={{0,64},{16,80},{32,96},{48,112},{64,0},{80,16},{96,32},{112,48},{1... | collective-permute-start | bytes 3080 | tf_op jit(solution)/shard_map/ppermute | solution.py:49
Sparse Core Ops, SparseCore 0:
  9.7 39.8 all-gather.1
